TPU v7x, 32 devices: a whole 2x2x4 slice. The times are simulated.
32 devices in a mesh: layer: 4 (over x, core), row: 4 (over z), col: 2 (over y).
Axes of the slice: x: 2, y: 2, z: 4, core: 2. Of those that a mesh axis runs over, the one named last changes fastest.
Arguments:
- sources: float32 [8, 256, 1024], P('layer', 'row', 'col'), may hold values from -14 to 14
- conduct: float32 [8, 256, 1024], P('layer', 'row', 'col'), may hold values from 0.5 to 4
- via_cond: float32 [8, 256, 1024], P('layer', 'row', 'col'), may hold values from 0.5 to 4
- via_map: int32 [8, 256, 1024], P('layer', 'row', 'col'), may hold values 0 or 1
- pad_map: int32 [256, 1024], P('row', 'col'), may hold values 0 or 1
- port_tile: int32 [4, 512], replicated, may hold values from 0 to 1023
- pivots: float32 [4, 512, 512], P(None, 'col'), may hold values from -1 to 2, as said below
- coupling: float32 [3, 512, 512], P(None, 'col'), may hold values from -0.109375 to 0.109375
Outputs:
- drop: float32 [8, 256, 1024], P('layer', 'row', 'col')
- ports: float32 [4, 512], replicated
Inputs may be any that keep to these rules, and one draw needn't show every extreme that they name: `pivots`: each block is symmetric.
All inputs are finite; a program needn't handle non-finite values. No bound on the sum of `via_map` or of `pad_map` on one device may be relied on, other than what follows from the above.
Results may differ from a plain program's by a relative error of at most 0.00023.
Values sent between devices are 32-bit elements; how exact they have to be, the bound alone decides.
No kernel may reach another device: no remote copies, remote signals or barrier semaphores. Data moves between devices by JAX's collectives and lax.ppermute only.
A program may use at most 64 MiB of HBM per device.

v0:
```python
import jax
import jax.numpy as jnp
from jax import lax
from jax.sharding import PartitionSpec as P

TILE = 16
PANEL = 512
NPANEL = 4
DEG = 3
ITERS = 2
pad_gain = 8.0
bound_low = 0.1
bound_high = 1.9
restrict_scale = 0.25
prolong_scale = 0.5


def padded(cells, sides, width):
    for axis, dim in sides:
        count = lax.axis_size(axis)
        ends = count - 1
        head = lax.slice_in_dim(cells, 0, width, axis=dim)
        tail = lax.slice_in_dim(cells, cells.shape[dim] - width, cells.shape[dim], axis=dim)
        cells = jnp.concatenate(
            [
                lax.ppermute(tail, axis, [(i, (i + 1) % count) for i in range(ends)]),
                cells,
                lax.ppermute(head, axis, [((i + 1) % count, i) for i in range(ends)]),
            ],
            axis=dim,
        )
    return cells


def shifted(grown):
    return (
        grown[2:, 1:-1, 1:-1],
        grown[:-2, 1:-1, 1:-1],
        grown[1:-1, 2:, 1:-1],
        grown[1:-1, :-2, 1:-1],
        grown[1:-1, 1:-1, 2:],
        grown[1:-1, 1:-1, :-2],
    )


def layer_grow(stack):
    return padded(stack, (("layer", 1), ("row", 2), ("col", 3)), 1)


def apply_grid(field, weights, pad_term, grow):
    grown = grow(field[None])[0]
    result = pad_term * field
    for weight, other in zip(weights, shifted(grown)):
        result = result + weight * (field - other)
    return result


def smooth(resid, weights, pad_term, inverse, grow):
    theta = (bound_high + bound_low) / 2.0
    delta = (bound_high - bound_low) / 2.0
    sigma = theta / delta
    rho = 1.0 / sigma
    change = inverse * resid / theta
    total = change
    for sweep in range(DEG - 1):
        remain = resid - apply_grid(total, weights, pad_term, grow)
        rho_new = 1.0 / (2.0 * sigma - rho)
        change = rho_new * rho * change + 2.0 * rho_new / delta * inverse * remain
        total = total + change
        rho = rho_new
    return total


def shards(sources, conduct, via_cond, via_map, pad_map, port_tile, pivots, coupling):
    highest = lax.Precision.HIGHEST
    layer_count = lax.axis_size("layer")
    vertical = via_cond * via_map.astype(jnp.float32)
    block_rows = sources.shape[1]
    currents, plane_cond, plane_vert = (sources, conduct, vertical)
    row_start = lax.axis_index("row") * block_rows
    top_flag = (lax.axis_index("layer") == layer_count - 1).astype(jnp.float32)
    local_layers, grid_rows, grid_cols = currents.shape
    grown = layer_grow(jnp.stack((plane_cond, plane_vert)))
    near_plane = shifted(grown[0])
    near_vert = shifted(grown[1])
    weights = (
        jnp.sqrt(plane_vert * near_vert[0]),
        jnp.sqrt(plane_vert * near_vert[1]),
        jnp.sqrt(plane_cond * near_plane[2]),
        jnp.sqrt(plane_cond * near_plane[3]),
        jnp.sqrt(plane_cond * near_plane[4]),
        jnp.sqrt(plane_cond * near_plane[5]),
    )
    top_layer = pad_gain * pad_map.astype(jnp.float32) * top_flag
    pad_term = jnp.concatenate(
        (jnp.zeros((local_layers - 1, grid_rows, grid_cols), jnp.float32), top_layer[None]), 0
    )
    diagonal = pad_term
    for weight in weights:
        diagonal = diagonal + weight
    inverse = 1.0 / diagonal
    total_tile_cols = grid_cols * lax.axis_size("col") // TILE
    row_tiles = (row_start + jnp.arange(grid_rows, dtype=jnp.int32)) // TILE
    col_tiles = (lax.axis_index("col") * grid_cols + jnp.arange(grid_cols, dtype=jnp.int32)) // TILE
    flat_tiles = port_tile.reshape(-1)
    row_select = (flat_tiles[:, None] // total_tile_cols == row_tiles[None, :]).astype(jnp.float32)
    col_select = (flat_tiles[:, None] % total_tile_cols == col_tiles[None, :]).astype(jnp.float32)
    share = PANEL // lax.axis_size("col")
    start = lax.axis_index("col") * share
    drop = jnp.zeros((local_layers, grid_rows, grid_cols), jnp.float32)
    ports = jnp.zeros((NPANEL, PANEL), jnp.float32)
    for outer in range(ITERS):
        resid = currents - apply_grid(drop, weights, pad_term, layer_grow)
        plane = jnp.sum(resid, axis=0)
        row_sums = jnp.dot(row_select, plane, precision=highest)
        local_rhs = jnp.sum(row_sums * col_select, axis=1).reshape(NPANEL, PANEL)
        rhs = lax.psum(local_rhs, ("layer", "row", "col")) * (restrict_scale / TILE)
        full = rhs[0]
        forward = [full]
        for section in range(1, NPANEL):
            piece = lax.dynamic_slice_in_dim(rhs[section], start, share) - jnp.dot(
                coupling[section - 1], full, precision=highest
            )
            full = lax.all_gather(piece, "col", axis=0, tiled=True)
            forward.append(full)
        scaled = [
            jnp.dot(pivots[section], forward[section], precision=highest)
            for section in range(NPANEL)
        ]
        results = [None] * NPANEL
        for section in range(NPANEL - 1, -1, -1):
            placed = lax.dynamic_update_slice_in_dim(
                jnp.zeros((PANEL,), jnp.float32), scaled[section], start, 0
            )
            if section < NPANEL - 1:
                later_rows = lax.dynamic_slice_in_dim(results[section + 1], start, share)
                placed = placed - jnp.dot(later_rows, coupling[section], precision=highest)
            results[section] = lax.psum(placed, "col")
        ports = jnp.stack(results)
        weighted_rows = jnp.transpose(row_select) * ports.reshape(-1)[None, :]
        field = jnp.dot(weighted_rows, col_select, precision=highest) * prolong_scale
        lifted = jnp.broadcast_to(field[None], (local_layers, grid_rows, grid_cols))
        drop = drop + lifted + smooth(resid, weights, pad_term, inverse, layer_grow)
    return (drop, ports)


def solution(mesh):
    placed = (
        P("layer", "row", "col"),
        P("layer", "row", "col"),
        P("layer", "row", "col"),
        P("layer", "row", "col"),
        P("row", "col"),
        P(),
        P(None, "col", None),
        P(None, "col", None),
    )
    return jax.shard_map(
        shards,
        mesh=mesh,
        in_specs=placed,
        out_specs=(P("layer", "row", "col"), P()),
        check_vma=False,
    )
```

profile of v0, /device:TPU:2, one launch (start us, length us, event | category | flops | bytes accessed | tf_op | source)
XLA Modules:
  0.0 358.2 jit_solution(15294549524432224454)
XLA Ops:
  0.7 2.1 collective-permute-start.7
  2.7 2.4 collective-permute-start.6
  7.2 1.9 collective-permute-start
  9.2 3.6 %collective-permute-start.1 = (f32[2,1,64,512]{3,2,1,0:T(8,128)S(1)}, f32[2,1,64,512]{3,2,1,0:T(8,128)S(1)}, u32[]{:S(2)}, u32[]{:S(2)}) collective-permute-start(f32[2,1,64,512]{3,2,1,0:T(8,128)S(1)} %get-tuple-element.41), channel_id=1, source_target_pairs={{8,0},{16,8},{24,16},{9,1},{17,9},{25,17},{10,2},{18,10},{26,18},{... | collective-permute-start | bytes 786440 | tf_op jit(solution)/shard_map/ppermute | solution.py:28
  13.1 3.5 collective-permute-start.8
  17.9 4.5 %collective-permute-start.2 = (f32[2,4,1,512]{3,2,1,0:T(1,128)S(1)}, f32[2,4,1,512]{3,2,1,0:T(1,128)S(1)}, u32[]{:S(2)}, u32[]{:S(2)}) collective-permute-start(f32[2,4,1,512]{3,2,1,0:T(1,128)S(1)} %get-tuple-element.16), channel_id=1, source_target_pairs={{0,2},{2,4},{4,6},{1,3},{3,5},{5,7},{8,10},{10,12},{12,14},{9,11},... | collective-permute-start | bytes 49160 | tf_op jit(solution)/shard_map/ppermute | solution.py:26
  23.9 3.4 collective-permute-start.10
  28.8 4.6 %collective-permute-start.4 = (f32[2,4,66,1]{3,2,1,0:T(8,128)S(1)}, f32[2,4,66,1]{3,2,1,0:T(8,128)S(1)}, u32[]{:S(2)}, u32[]{:S(2)}) collective-permute-start(f32[2,4,66,1]{3,2,1,0:T(8,128)S(1)} %get-tuple-element.14), channel_id=1, source_target_pairs={{0,1},{2,3},{4,5},{6,7},{8,9},{10,11},{12,13},{14,15},{16,17},{18,... | collective-permute-start | bytes 6344 | tf_op jit(solution)/shard_map/ppermute | solution.py:26
  35.1 2.5 collective-permute-done.4
  37.6 4.4 %collective-permute-done.5 = f32[2,4,66,1]{3,2,1,0:T(8,128)S(1)} collective-permute-done((f32[2,4,66,1]{3,2,1,0:T(8,128)S(1)}, f32[2,4,66,1]{3,2,1,0:T(8,128)S(1)}, u32[]{:S(2)}, u32[]{:S(2)}) %collective-permute-start.5) | collective-permute-done | bytes 2144 | tf_op jit(solution)/shard_map/ppermute | solution.py:28
  43.8 1.7 fusion.211
  45.5 2.6 fusion.4
  48.1 41.7 %psum.70 = f32[4,512]{1,0:T(4,128)S(1)} all-reduce(f32[4,512]{1,0:T(4,128)S(1)} %reshape.145), channel_id=1, replica_groups=mesh['layer'=4,'row'=4,'col'=2] {'layer','row','col'}, use_global_device_ids=true, to_apply=%region_2.3 | all-reduce | flops 2048 | bytes 16384 | tf_op jit(solution)/shard_map/psum | solution.py:117
  90.4 2.2 fusion.56
  92.6 4.2 %all-gather = f32[2,1,256]{2,1,0:T(1,128)S(1)} all-gather(f32[1,1,256]{2,1,0:T(1,128)S(1)} %bitcast.242), channel_id=1, replica_groups=mesh['layer'=4,'row'=4,'col'=2] {'col'}, dimensions={0}, use_global_device_ids=true | all-gather | bytes 3072 | tf_op jit(solution)/shard_map/all_gather | solution.py:124
  97.4 4.2 %all-gather.1 = f32[2,1,256]{2,1,0:T(1,128)S(1)} all-gather(f32[1,1,256]{2,1,0:T(1,128)S(1)} %bitcast.243), channel_id=1, replica_groups=mesh['layer'=4,'row'=4,'col'=2] {'col'}, dimensions={0}, use_global_device_ids=true | all-gather | bytes 3072 | tf_op jit(solution)/shard_map/all_gather | solution.py:124
  102.7 4.2 %all-gather.2 = f32[2,1,256]{2,1,0:T(1,128)S(1)} all-gather(f32[1,1,256]{2,1,0:T(1,128)S(1)} %bitcast.244), channel_id=1, replica_groups=mesh['layer'=4,'row'=4,'col'=2] {'col'}, dimensions={0}, use_global_device_ids=true | all-gather | bytes 3072 | tf_op jit(solution)/shard_map/all_gather | solution.py:124
  107.7 4.9 %psum.71 = f32[512]{0:T(512)S(1)} all-reduce(f32[512]{0:T(512)S(1)} %dynamic_update_slice.27), channel_id=1, replica_groups=mesh['layer'=4,'row'=4,'col'=2] {'col'}, use_global_device_ids=true, to_apply=%region_3.4 | all-reduce | flops 512 | bytes 4096 | tf_op jit(solution)/shard_map/psum | solution.py:138
  113.3 4.9 %psum.72 = f32[512]{0:T(512)S(1)} all-reduce(f32[512]{0:T(512)S(1)} %sub.193), channel_id=1, replica_groups=mesh['layer'=4,'row'=4,'col'=2] {'col'}, use_global_device_ids=true, to_apply=%region_4.5 | all-reduce | flops 512 | bytes 4096 | tf_op jit(solution)/shard_map/psum | solution.py:138
  119.9 1.9 collective-permute-start.12
  121.9 3.6 %collective-permute-start.13 = (f32[1,1,64,512]{3,2,1,0:T(8,128)S(1)}, f32[1,1,64,512]{3,2,1,0:T(8,128)S(1)}, u32[]{:S(2)}, u32[]{:S(2)}) collective-permute-start(f32[1,1,64,512]{3,2,1,0:T(8,128)S(1)} %get-tuple-element.53), channel_id=1, source_target_pairs={{8,0},{16,8},{24,16},{9,1},{17,9},{25,17},{10,2},{18,10},{26,18},{... | collective-permute-start | bytes 393224 | tf_op jit(solution)/shard_map/ppermute | solution.py:28
  125.5 2.1 fusion.44
  128.0 3.4 collective-permute-start.14
  133.9 3.1 collective-permute-done.15
  137.8 3.1 collective-permute-start.16
  142.2 6.3 %psum.73 = f32[512]{0:T(512)S(1)} all-reduce(f32[512]{0:T(512)S(1)} %sub.194), channel_id=1, replica_groups=mesh['layer'=4,'row'=4,'col'=2] {'col'}, use_global_device_ids=true, to_apply=%region_5.6 | all-reduce | flops 512 | bytes 4096 | tf_op jit(solution)/shard_map/psum | solution.py:138
  152.8 1.7 fusion.196
  155.9 1.9 collective-permute-start.18
  157.8 3.6 %collective-permute-start.19 = (f32[1,1,64,512]{3,2,1,0:T(8,128)}, f32[1,1,64,512]{3,2,1,0:T(8,128)}, u32[]{:S(2)}, u32[]{:S(2)}) collective-permute-start(f32[1,1,64,512]{3,2,1,0:T(8,128)} %get-tuple-element.51), channel_id=1, source_target_pairs={{8,0},{16,8},{24,16},{9,1},{17,9},{25,17},{10,2},{18,10},{26,18},{... | collective-permute-start | bytes 393224 | tf_op jit(solution)/shard_map/ppermute | solution.py:28
  161.9 4.9 %psum.74 = f32[1,512]{1,0:T(1,128)S(1)} all-reduce(f32[1,512]{1,0:T(1,128)S(1)} %bitcast.217), channel_id=1, replica_groups=mesh['layer'=4,'row'=4,'col'=2] {'col'}, use_global_device_ids=true, to_apply=%region_6.7 | all-reduce | flops 512 | bytes 4096 | tf_op jit(solution)/shard_map/psum | solution.py:138
  167.7 3.3 collective-permute-start.20
  172.4 4.2 %collective-permute-done.21 = f32[1,4,1,512]{3,2,1,0:T(1,128)S(1)} collective-permute-done((f32[1,4,1,512]{3,2,1,0:T(1,128)S(1)}, f32[1,4,1,512]{3,2,1,0:T(1,128)S(1)}, u32[]{:S(2)}, u32[]{:S(2)}) %collective-permute-start.21) | collective-permute-done | bytes 8224 | tf_op jit(solution)/shard_map/ppermute | solution.py:28
  177.6 4.0 %collective-permute-start.22 = (f32[1,4,66,1]{3,2,1,0:T(8,128)S(1)}, f32[1,4,66,1]{3,2,1,0:T(8,128)S(1)}, u32[]{:S(2)}, u32[]{:S(2)}) collective-permute-start(f32[1,4,66,1]{3,2,1,0:T(8,128)S(1)} %get-tuple-element.24), channel_id=1, source_target_pairs={{0,1},{2,3},{4,5},{6,7},{8,9},{10,11},{12,13},{14,15},{16,17},{18,... | collective-permute-start | bytes 3176 | tf_op jit(solution)/shard_map/ppermute | solution.py:26
  182.9 2.2 fusion.12
  185.1 3.5 collective-permute-done.23
  191.0 2.1 collective-permute-start.24
  193.0 3.6 %collective-permute-start.25 = (f32[1,1,64,512]{3,2,1,0:T(8,128)S(1)}, f32[1,1,64,512]{3,2,1,0:T(8,128)S(1)}, u32[]{:S(2)}, u32[]{:S(2)}) collective-permute-start(f32[1,1,64,512]{3,2,1,0:T(8,128)S(1)} %get-tuple-element.49), channel_id=1, source_target_pairs={{8,0},{16,8},{24,16},{9,1},{17,9},{25,17},{10,2},{18,10},{26,18},{... | collective-permute-start | bytes 393224 | tf_op jit(solution)/shard_map/ppermute | solution.py:28
  197.4 1.8 collective-permute-done.25
  199.2 2.4 collective-permute-start.26
  202.9 4.2 %collective-permute-done.27 = f32[1,4,1,512]{3,2,1,0:T(1,128)S(1)} collective-permute-done((f32[1,4,1,512]{3,2,1,0:T(1,128)S(1)}, f32[1,4,1,512]{3,2,1,0:T(1,128)S(1)}, u32[]{:S(2)}, u32[]{:S(2)}) %collective-permute-start.27) | collective-permute-done | bytes 8224 | tf_op jit(solution)/shard_map/ppermute | solution.py:28
  211.3 4.4 %collective-permute-done.29 = f32[1,4,66,1]{3,2,1,0:T(8,128)S(1)} collective-permute-done((f32[1,4,66,1]{3,2,1,0:T(8,128)S(1)}, f32[1,4,66,1]{3,2,1,0:T(8,128)S(1)}, u32[]{:S(2)}, u32[]{:S(2)}) %collective-permute-start.29) | collective-permute-done | bytes 1088 | tf_op jit(solution)/shard_map/ppermute | solution.py:28
  217.2 2.5 fusion.5
  219.8 38.1 %psum.75 = f32[4,512]{1,0:T(4,128)S(1)} all-reduce(f32[4,512]{1,0:T(4,128)S(1)} %reshape.146), channel_id=1, replica_groups=mesh['layer'=4,'row'=4,'col'=2] {'layer','row','col'}, use_global_device_ids=true, to_apply=%region_9.10 | all-reduce | flops 2048 | bytes 16384 | tf_op jit(solution)/shard_map/psum | solution.py:117
  258.5 2.2 fusion.54
  260.8 4.2 %all-gather.3 = f32[2,1,256]{2,1,0:T(1,128)S(1)} all-gather(f32[1,1,256]{2,1,0:T(1,128)S(1)} %bitcast.245), channel_id=1, replica_groups=mesh['layer'=4,'row'=4,'col'=2] {'col'}, dimensions={0}, use_global_device_ids=true | all-gather | bytes 3072 | tf_op jit(solution)/shard_map/all_gather | solution.py:124
  265.5 4.2 %all-gather.4 = f32[2,1,256]{2,1,0:T(1,128)S(1)} all-gather(f32[1,1,256]{2,1,0:T(1,128)S(1)} %bitcast.246), channel_id=1, replica_groups=mesh['layer'=4,'row'=4,'col'=2] {'col'}, dimensions={0}, use_global_device_ids=true | all-gather | bytes 3072 | tf_op jit(solution)/shard_map/all_gather | solution.py:124
  270.8 4.2 %all-gather.5 = f32[2,1,256]{2,1,0:T(1,128)S(1)} all-gather(f32[1,1,256]{2,1,0:T(1,128)S(1)} %bitcast.247), channel_id=1, replica_groups=mesh['layer'=4,'row'=4,'col'=2] {'col'}, dimensions={0}, use_global_device_ids=true | all-gather | bytes 3072 | tf_op jit(solution)/shard_map/all_gather | solution.py:124
  275.8 4.9 %psum.76 = f32[512]{0:T(512)S(1)} all-reduce(f32[512]{0:T(512)S(1)} %dynamic_update_slice.31), channel_id=1, replica_groups=mesh['layer'=4,'row'=4,'col'=2] {'col'}, use_global_device_ids=true, to_apply=%region_10.11 | all-reduce | flops 512 | bytes 4096 | tf_op jit(solution)/shard_map/psum | solution.py:138
  281.4 5.1 %psum.77 = f32[512]{0:T(512)S(1)} all-reduce(f32[512]{0:T(512)S(1)} %sub.220), channel_id=1, replica_groups=mesh['layer'=4,'row'=4,'col'=2] {'col'}, use_global_device_ids=true, to_apply=%region_11.12 | all-reduce | flops 512 | bytes 4096 | tf_op jit(solution)/shard_map/psum | solution.py:138
  288.3 1.9 collective-permute-start.30
  290.2 3.6 %collective-permute-start.31 = (f32[1,1,64,512]{3,2,1,0:T(8,128)S(1)}, f32[1,1,64,512]{3,2,1,0:T(8,128)S(1)}, u32[]{:S(2)}, u32[]{:S(2)}) collective-permute-start(f32[1,1,64,512]{3,2,1,0:T(8,128)S(1)} %get-tuple-element.47), channel_id=1, source_target_pairs={{8,0},{16,8},{24,16},{9,1},{17,9},{25,17},{10,2},{18,10},{26,18},{... | collective-permute-start | bytes 393224 | tf_op jit(solution)/shard_map/ppermute | solution.py:28
  293.8 2.1 fusion.42
  296.4 3.8 %collective-permute-start.32 = (f32[1,4,1,512]{3,2,1,0:T(1,128)S(1)}, f32[1,4,1,512]{3,2,1,0:T(1,128)S(1)}, u32[]{:S(2)}, u32[]{:S(2)}) collective-permute-start(f32[1,4,1,512]{3,2,1,0:T(1,128)S(1)} %get-tuple-element.32), channel_id=1, source_target_pairs={{0,2},{2,4},{4,6},{1,3},{3,5},{5,7},{8,10},{10,12},{12,14},{9,11},... | collective-permute-start | bytes 24584 | tf_op jit(solution)/shard_map/ppermute | solution.py:26
  302.7 3.1 collective-permute-done.33
  306.5 3.9 %collective-permute-start.34 = (f32[1,4,66,1]{3,2,1,0:T(8,128)}, f32[1,4,66,1]{3,2,1,0:T(8,128)S(1)}, u32[]{:S(2)}, u32[]{:S(2)}) collective-permute-start(f32[1,4,66,1]{3,2,1,0:T(8,128)} %get-tuple-element.20), channel_id=1, source_target_pairs={{0,1},{2,3},{4,5},{6,7},{8,9},{10,11},{12,13},{14,15},{16,17},{18,... | collective-permute-start | bytes 3176 | tf_op jit(solution)/shard_map/ppermute | solution.py:26
  311.7 6.2 %psum.78 = f32[512]{0:T(512)S(1)} all-reduce(f32[512]{0:T(512)S(1)} %sub.221), channel_id=1, replica_groups=mesh['layer'=4,'row'=4,'col'=2] {'col'}, use_global_device_ids=true, to_apply=%region_12.13 | all-reduce | flops 512 | bytes 4096 | tf_op jit(solution)/shard_map/psum | solution.py:138
  323.1 1.9 collective-permute-start.36
  325.0 3.6 %collective-permute-start.37 = (f32[1,1,64,512]{3,2,1,0:T(8,128)}, f32[1,1,64,512]{3,2,1,0:T(8,128)}, u32[]{:S(2)}, u32[]{:S(2)}) collective-permute-start(f32[1,1,64,512]{3,2,1,0:T(8,128)} %get-tuple-element.45), channel_id=1, source_target_pairs={{8,0},{16,8},{24,16},{9,1},{17,9},{25,17},{10,2},{18,10},{26,18},{... | collective-permute-start | bytes 393224 | tf_op jit(solution)/shard_map/ppermute | solution.py:28
  329.3 4.9 %psum.79 = f32[1,512]{1,0:T(1,128)S(1)} all-reduce(f32[1,512]{1,0:T(1,128)S(1)} %bitcast.218), channel_id=1, replica_groups=mesh['layer'=4,'row'=4,'col'=2] {'col'}, use_global_device_ids=true, to_apply=%region_13.14 | all-reduce | flops 512 | bytes 4096 | tf_op jit(solution)/shard_map/psum | solution.py:138
  335.2 2.6 collective-permute-start.38
  339.1 2.2 fusion.15
  341.3 2.0 collective-permute-done.39
  344.2 4.0 %collective-permute-start.40 = (f32[1,4,66,1]{3,2,1,0:T(8,128)S(1)}, f32[1,4,66,1]{3,2,1,0:T(8,128)S(1)}, u32[]{:S(2)}, u32[]{:S(2)}) collective-permute-start(f32[1,4,66,1]{3,2,1,0:T(8,128)S(1)} %get-tuple-element.18), channel_id=1, source_target_pairs={{0,1},{2,3},{4,5},{6,7},{8,9},{10,11},{12,13},{14,15},{16,17},{18,... | collective-permute-start | bytes 3176 | tf_op jit(solution)/shard_map/ppermute | solution.py:26
  350.8 4.4 %collective-permute-done.41 = f32[1,4,66,1]{3,2,1,0:T(8,128)S(1)} collective-permute-done((f32[1,4,66,1]{3,2,1,0:T(8,128)S(1)}, f32[1,4,66,1]{3,2,1,0:T(8,128)S(1)}, u32[]{:S(2)}, u32[]{:S(2)}) %collective-permute-start.41) | collective-permute-done | bytes 1088 | tf_op jit(solution)/shard_map/ppermute | solution.py:28
  (281 shorter events, 65.3 us)
Async XLA Ops:
  0.7 12.3 %collective-permute-start.7 = (f32[1,1,64,512]{3,2,1,0:T(8,128)S(1)}, f32[1,1,64,512]{3,2,1,0:T(8,128)S(1)}, u32[]{:S(2)}, u32[]{:S(2)}) collective-permute-start(f32[1,1,64,512]{3,2,1,0:T(8,128)S(1)} %broadcast.185), channel_id=1, source_target_pairs={{8,0},{16,8},{24,16},{9,1},{17,9},{25,17},{10,2},{18,10},{26,18},{... | collective-permute-start | bytes 393224 | tf_op jit(solution)/shard_map/ppermute | solution.py:28
  2.7 10.3 %collective-permute-start.6 = (f32[1,1,64,512]{3,2,1,0:T(8,128)S(1)}, f32[1,1,64,512]{3,2,1,0:T(8,128)S(1)}, u32[]{:S(2)}, u32[]{:S(2)}) collective-permute-start(f32[1,1,64,512]{3,2,1,0:T(8,128)S(1)} %broadcast.185), channel_id=1, source_target_pairs={{0,8},{8,16},{16,24},{1,9},{9,17},{17,25},{2,10},{10,18},{18,26},{... | collective-permute-start | bytes 393224 | tf_op jit(solution)/shard_map/ppermute | solution.py:26
  7.2 10.6 %collective-permute-start = (f32[2,1,64,512]{3,2,1,0:T(8,128)S(1)}, f32[2,1,64,512]{3,2,1,0:T(8,128)S(1)}, u32[]{:S(2)}, u32[]{:S(2)}) collective-permute-start(f32[2,1,64,512]{3,2,1,0:T(8,128)S(1)} %get-tuple-element.40), channel_id=1, source_target_pairs={{0,8},{8,16},{16,24},{1,9},{9,17},{17,25},{2,10},{10,18},{18,26},{... | collective-permute-start | bytes 786440 | tf_op jit(solution)/shard_map/ppermute | solution.py:26
  9.2 8.7 %collective-permute-start.1 = (f32[2,1,64,512]{3,2,1,0:T(8,128)S(1)}, f32[2,1,64,512]{3,2,1,0:T(8,128)S(1)}, u32[]{:S(2)}, u32[]{:S(2)}) collective-permute-start(f32[2,1,64,512]{3,2,1,0:T(8,128)S(1)} %get-tuple-element.41), channel_id=1, source_target_pairs={{8,0},{16,8},{24,16},{9,1},{17,9},{25,17},{10,2},{18,10},{26,18},{... | collective-permute-start | bytes 786440 | tf_op jit(solution)/shard_map/ppermute | solution.py:28
  12.9 32.6 %copy-start.46 = (s32[2048]{0:T(1024)}, s32[2048]{0:T(1024)S(1)}, u32[]{:S(2)}) copy-start(s32[2048]{0:T(1024)S(1)} %get-tuple-element.60) | copy-start | bytes 24580
  12.9 32.6 %copy-start.49 = (s32[2048]{0:T(1024)}, s32[2048]{0:T(1024)S(1)}, u32[]{:S(2)}) copy-start(s32[2048]{0:T(1024)S(1)} %get-tuple-element.61) | copy-start | bytes 24580
  12.9 32.6 %copy-start.60 = (s32[64]{0:T(128)}, s32[64]{0:T(128)S(1)}, u32[]{:S(2)}) copy-start(s32[64]{0:T(128)S(1)} %and_select_fusion) | copy-start | bytes 772
  13.0 32.5 %copy-start.57 = (s32[512]{0:T(512)}, s32[512]{0:T(512)S(1)}, u32[]{:S(2)}) copy-start(s32[512]{0:T(512)S(1)} %add_select_fusion.2) | copy-start | bytes 6148
  13.1 10.7 %collective-permute-start.8 = (f32[1,4,1,512]{3,2,1,0:T(1,128)S(1)}, f32[1,4,1,512]{3,2,1,0:T(1,128)S(1)}, u32[]{:S(2)}, u32[]{:S(2)}) collective-permute-start(f32[1,4,1,512]{3,2,1,0:T(1,128)S(1)} %get-tuple-element.42), channel_id=1, source_target_pairs={{0,2},{2,4},{4,6},{1,3},{3,5},{5,7},{8,10},{10,12},{12,14},{9,11},... | collective-permute-start | bytes 24584 | tf_op jit(solution)/shard_map/ppermute | solution.py:26
  16.5 7.2 %collective-permute-start.9 = (f32[1,4,1,512]{3,2,1,0:T(1,128)S(1)}, f32[1,4,1,512]{3,2,1,0:T(1,128)S(1)}, u32[]{:S(2)}, u32[]{:S(2)}) collective-permute-start(f32[1,4,1,512]{3,2,1,0:T(1,128)S(1)} %get-tuple-element.43), channel_id=1, source_target_pairs={{2,0},{4,2},{6,4},{3,1},{5,3},{7,5},{10,8},{12,10},{14,12},{11,9},... | collective-permute-start | bytes 24584 | tf_op jit(solution)/shard_map/ppermute | solution.py:28
  17.9 10.7 %collective-permute-start.2 = (f32[2,4,1,512]{3,2,1,0:T(1,128)S(1)}, f32[2,4,1,512]{3,2,1,0:T(1,128)S(1)}, u32[]{:S(2)}, u32[]{:S(2)}) collective-permute-start(f32[2,4,1,512]{3,2,1,0:T(1,128)S(1)} %get-tuple-element.16), channel_id=1, source_target_pairs={{0,2},{2,4},{4,6},{1,3},{3,5},{5,7},{8,10},{10,12},{12,14},{9,11},... | collective-permute-start | bytes 49160 | tf_op jit(solution)/shard_map/ppermute | solution.py:26
  22.5 6.2 %collective-permute-start.3 = (f32[2,4,1,512]{3,2,1,0:T(1,128)S(1)}, f32[2,4,1,512]{3,2,1,0:T(1,128)S(1)}, u32[]{:S(2)}, u32[]{:S(2)}) collective-permute-start(f32[2,4,1,512]{3,2,1,0:T(1,128)S(1)} %get-tuple-element.17), channel_id=1, source_target_pairs={{2,0},{4,2},{6,4},{3,1},{5,3},{7,5},{10,8},{12,10},{14,12},{11,9},... | collective-permute-start | bytes 49160 | tf_op jit(solution)/shard_map/ppermute | solution.py:28
  23.9 10.8 %collective-permute-start.10 = (f32[1,4,66,1]{3,2,1,0:T(8,128)S(1)}, f32[1,4,66,1]{3,2,1,0:T(8,128)S(1)}, u32[]{:S(2)}, u32[]{:S(2)}) collective-permute-start(f32[1,4,66,1]{3,2,1,0:T(8,128)S(1)} %get-tuple-element.28), channel_id=1, source_target_pairs={{0,1},{2,3},{4,5},{6,7},{8,9},{10,11},{12,13},{14,15},{16,17},{18,... | collective-permute-start | bytes 3176 | tf_op jit(solution)/shard_map/ppermute | solution.py:26
  27.4 7.4 %collective-permute-start.11 = (f32[1,4,66,1]{3,2,1,0:T(8,128)S(1)}, f32[1,4,66,1]{3,2,1,0:T(8,128)S(1)}, u32[]{:S(2)}, u32[]{:S(2)}) collective-permute-start(f32[1,4,66,1]{3,2,1,0:T(8,128)S(1)} %get-tuple-element.29), channel_id=1, source_target_pairs={{1,0},{3,2},{5,4},{7,6},{9,8},{11,10},{13,12},{15,14},{17,16},{19,... | collective-permute-start | bytes 3176 | tf_op jit(solution)/shard_map/ppermute | solution.py:28
  28.8 8.8 %collective-permute-start.4 = (f32[2,4,66,1]{3,2,1,0:T(8,128)S(1)}, f32[2,4,66,1]{3,2,1,0:T(8,128)S(1)}, u32[]{:S(2)}, u32[]{:S(2)}) collective-permute-start(f32[2,4,66,1]{3,2,1,0:T(8,128)S(1)} %get-tuple-element.14), channel_id=1, source_target_pairs={{0,1},{2,3},{4,5},{6,7},{8,9},{10,11},{12,13},{14,15},{16,17},{18,... | collective-permute-start | bytes 6344 | tf_op jit(solution)/shard_map/ppermute | solution.py:26
  33.4 8.6 %collective-permute-start.5 = (f32[2,4,66,1]{3,2,1,0:T(8,128)S(1)}, f32[2,4,66,1]{3,2,1,0:T(8,128)S(1)}, u32[]{:S(2)}, u32[]{:S(2)}) collective-permute-start(f32[2,4,66,1]{3,2,1,0:T(8,128)S(1)} %get-tuple-element.15), channel_id=1, source_target_pairs={{1,0},{3,2},{5,4},{7,6},{9,8},{11,10},{13,12},{15,14},{17,16},{19,... | collective-permute-start | bytes 6344 | tf_op jit(solution)/shard_map/ppermute | solution.py:28
  45.5 73.3 %copy-start.1 = (f32[2,64,512]{2,1,0:T(8,128)}, f32[2,64,512]{2,1,0:T(8,128)S(1)}, u32[]{:S(2)}) copy-start(f32[2,64,512]{2,1,0:T(8,128)S(1)} %get-tuple-element.10) | copy-start | bytes 786436
  45.5 73.3 %copy-start.5 = (f32[2,64,512]{2,1,0:T(8,128)}, f32[2,64,512]{2,1,0:T(8,128)S(1)}, u32[]{:S(2)}) copy-start(f32[2,64,512]{2,1,0:T(8,128)S(1)} %get-tuple-element.11) | copy-start | bytes 786436
  45.5 44.4 %copy-start = (f32[3,256,512]{2,1,0:T(8,128)S(1)}, f32[3,256,512]{2,1,0:T(8,128)}, u32[]{:S(2)}) copy-start(f32[3,256,512]{2,1,0:T(8,128)} %param.15) | copy-start | bytes 4718596
  119.9 30.1 %copy-start.14 = (f32[1,2,64,512]{3,2,1,0:T(8,128)}, f32[1,2,64,512]{3,2,1,0:T(8,128)S(1)}, u32[]{:S(2)}) copy-start(f32[1,2,64,512]{3,2,1,0:T(8,128)S(1)} %fusion.208) | copy-start | bytes 786436
  119.9 7.7 %collective-permute-start.12 = (f32[1,1,64,512]{3,2,1,0:T(8,128)S(1)}, f32[1,1,64,512]{3,2,1,0:T(8,128)S(1)}, u32[]{:S(2)}, u32[]{:S(2)}) collective-permute-start(f32[1,1,64,512]{3,2,1,0:T(8,128)S(1)} %get-tuple-element.52), channel_id=1, source_target_pairs={{0,8},{8,16},{16,24},{1,9},{9,17},{17,25},{2,10},{10,18},{18,26},{... | collective-permute-start | bytes 393224 | tf_op jit(solution)/shard_map/ppermute | solution.py:26
  121.9 6.1 %collective-permute-start.13 = (f32[1,1,64,512]{3,2,1,0:T(8,128)S(1)}, f32[1,1,64,512]{3,2,1,0:T(8,128)S(1)}, u32[]{:S(2)}, u32[]{:S(2)}) collective-permute-start(f32[1,1,64,512]{3,2,1,0:T(8,128)S(1)} %get-tuple-element.53), channel_id=1, source_target_pairs={{8,0},{16,8},{24,16},{9,1},{17,9},{25,17},{10,2},{18,10},{26,18},{... | collective-permute-start | bytes 393224 | tf_op jit(solution)/shard_map/ppermute | solution.py:28
  127.6 22.4 %copy-start.23 = (f32[1,1,64,512]{3,2,1,0:T(8,128)}, f32[1,1,64,512]{3,2,1,0:T(8,128)S(1)}, u32[]{:S(2)}) copy-start(f32[1,1,64,512]{3,2,1,0:T(8,128)S(1)} %collective-permute-done.12) | copy-start | bytes 393220
  128.0 22.0 %copy-start.24 = (f32[1,1,64,512]{3,2,1,0:T(8,128)}, f32[1,1,64,512]{3,2,1,0:T(8,128)S(1)}, u32[]{:S(2)}) copy-start(f32[1,1,64,512]{3,2,1,0:T(8,128)S(1)} %collective-permute-done.13) | copy-start | bytes 393220
  128.0 5.9 %collective-permute-start.14 = (f32[1,4,1,512]{3,2,1,0:T(1,128)S(1)}, f32[1,4,1,512]{3,2,1,0:T(1,128)S(1)}, u32[]{:S(2)}, u32[]{:S(2)}) collective-permute-start(f32[1,4,1,512]{3,2,1,0:T(1,128)S(1)} %get-tuple-element.38), channel_id=1, source_target_pairs={{0,2},{2,4},{4,6},{1,3},{3,5},{5,7},{8,10},{10,12},{12,14},{9,11},... | collective-permute-start | bytes 24584 | tf_op jit(solution)/shard_map/ppermute | solution.py:26
  131.5 5.5 %collective-permute-start.15 = (f32[1,4,1,512]{3,2,1,0:T(1,128)S(1)}, f32[1,4,1,512]{3,2,1,0:T(1,128)S(1)}, u32[]{:S(2)}, u32[]{:S(2)}) collective-permute-start(f32[1,4,1,512]{3,2,1,0:T(1,128)S(1)} %get-tuple-element.39), channel_id=1, source_target_pairs={{2,0},{4,2},{6,4},{3,1},{5,3},{7,5},{10,8},{12,10},{14,12},{11,9},... | collective-permute-start | bytes 24584 | tf_op jit(solution)/shard_map/ppermute | solution.py:28
  137.8 12.2 %collective-permute-start.16 = (f32[1,4,66,1]{3,2,1,0:T(8,128)}, f32[1,4,66,1]{3,2,1,0:T(8,128)S(1)}, u32[]{:S(2)}, u32[]{:S(2)}) collective-permute-start(f32[1,4,66,1]{3,2,1,0:T(8,128)} %get-tuple-element.26), channel_id=1, source_target_pairs={{0,1},{2,3},{4,5},{6,7},{8,9},{10,11},{12,13},{14,15},{16,17},{18,... | collective-permute-start | bytes 3176 | tf_op jit(solution)/shard_map/ppermute | solution.py:26
  140.9 10.3 %collective-permute-start.17 = (f32[1,4,66,1]{3,2,1,0:T(8,128)}, f32[1,4,66,1]{3,2,1,0:T(8,128)}, u32[]{:S(2)}, u32[]{:S(2)}) collective-permute-start(f32[1,4,66,1]{3,2,1,0:T(8,128)} %get-tuple-element.27), channel_id=1, source_target_pairs={{1,0},{3,2},{5,4},{7,6},{9,8},{11,10},{13,12},{15,14},{17,16},{19,... | collective-permute-start | bytes 3176 | tf_op jit(solution)/shard_map/ppermute | solution.py:28
  155.2 27.7 %copy-start.47 = (s32[2048]{0:T(1024)S(1)}, s32[2048]{0:T(1024)}, u32[]{:S(2)}) copy-start(s32[2048]{0:T(1024)} %copy-done.46) | copy-start | bytes 24580
  155.2 27.7 %copy-start.50 = (s32[2048]{0:T(1024)S(1)}, s32[2048]{0:T(1024)}, u32[]{:S(2)}) copy-start(s32[2048]{0:T(1024)} %copy-done.49) | copy-start | bytes 24580
  155.2 27.7 %copy-start.58 = (s32[512]{0:T(512)S(1)}, s32[512]{0:T(512)}, u32[]{:S(2)}) copy-start(s32[512]{0:T(512)} %copy-done.57) | copy-start | bytes 6148
  155.2 27.7 %copy-start.61 = (s32[64]{0:T(128)S(1)}, s32[64]{0:T(128)}, u32[]{:S(2)}) copy-start(s32[64]{0:T(128)} %copy-done.60) | copy-start | bytes 772
  155.9 10.9 %collective-permute-start.18 = (f32[1,1,64,512]{3,2,1,0:T(8,128)}, f32[1,1,64,512]{3,2,1,0:T(8,128)}, u32[]{:S(2)}, u32[]{:S(2)}) collective-permute-start(f32[1,1,64,512]{3,2,1,0:T(8,128)} %get-tuple-element.50), channel_id=1, source_target_pairs={{0,8},{8,16},{16,24},{1,9},{9,17},{17,25},{2,10},{10,18},{18,26},{... | collective-permute-start | bytes 393224 | tf_op jit(solution)/shard_map/ppermute | solution.py:26
  157.8 9.0 %collective-permute-start.19 = (f32[1,1,64,512]{3,2,1,0:T(8,128)}, f32[1,1,64,512]{3,2,1,0:T(8,128)}, u32[]{:S(2)}, u32[]{:S(2)}) collective-permute-start(f32[1,1,64,512]{3,2,1,0:T(8,128)} %get-tuple-element.51), channel_id=1, source_target_pairs={{8,0},{16,8},{24,16},{9,1},{17,9},{25,17},{10,2},{18,10},{26,18},{... | collective-permute-start | bytes 393224 | tf_op jit(solution)/shard_map/ppermute | solution.py:28
  166.8 21.8 %copy-start.20 = (f32[1,2,64,512]{3,2,1,0:T(8,128)S(1)}, f32[1,2,64,512]{3,2,1,0:T(8,128)}, u32[]{:S(2)}) copy-start(f32[1,2,64,512]{3,2,1,0:T(8,128)} %copy-done.19) | copy-start | bytes 786436
  167.7 4.7 %collective-permute-start.20 = (f32[1,4,1,512]{3,2,1,0:T(1,128)S(1)}, f32[1,4,1,512]{3,2,1,0:T(1,128)S(1)}, u32[]{:S(2)}, u32[]{:S(2)}) collective-permute-start(f32[1,4,1,512]{3,2,1,0:T(1,128)S(1)} %get-tuple-element.36), channel_id=1, source_target_pairs={{0,2},{2,4},{4,6},{1,3},{3,5},{5,7},{8,10},{10,12},{12,14},{9,11},... | collective-permute-start | bytes 24584 | tf_op jit(solution)/shard_map/ppermute | solution.py:26
  171.0 5.5 %collective-permute-start.21 = (f32[1,4,1,512]{3,2,1,0:T(1,128)S(1)}, f32[1,4,1,512]{3,2,1,0:T(1,128)S(1)}, u32[]{:S(2)}, u32[]{:S(2)}) collective-permute-start(f32[1,4,1,512]{3,2,1,0:T(1,128)S(1)} %get-tuple-element.37), channel_id=1, source_target_pairs={{2,0},{4,2},{6,4},{3,1},{5,3},{7,5},{10,8},{12,10},{14,12},{11,9},... | collective-permute-start | bytes 24584 | tf_op jit(solution)/shard_map/ppermute | solution.py:28
  177.6 7.5 %collective-permute-start.22 = (f32[1,4,66,1]{3,2,1,0:T(8,128)S(1)}, f32[1,4,66,1]{3,2,1,0:T(8,128)S(1)}, u32[]{:S(2)}, u32[]{:S(2)}) collective-permute-start(f32[1,4,66,1]{3,2,1,0:T(8,128)S(1)} %get-tuple-element.24), channel_id=1, source_target_pairs={{0,1},{2,3},{4,5},{6,7},{8,9},{10,11},{12,13},{14,15},{16,17},{18,... | collective-permute-start | bytes 3176 | tf_op jit(solution)/shard_map/ppermute | solution.py:26
  181.5 7.0 %collective-permute-start.23 = (f32[1,4,66,1]{3,2,1,0:T(8,128)S(1)}, f32[1,4,66,1]{3,2,1,0:T(8,128)S(1)}, u32[]{:S(2)}, u32[]{:S(2)}) collective-permute-start(f32[1,4,66,1]{3,2,1,0:T(8,128)S(1)} %get-tuple-element.25), channel_id=1, source_target_pairs={{1,0},{3,2},{5,4},{7,6},{9,8},{11,10},{13,12},{15,14},{17,16},{19,... | collective-permute-start | bytes 3176 | tf_op jit(solution)/shard_map/ppermute | solution.py:28
  190.9 25.2 %copy-start.9 = (f32[2,64,512]{2,1,0:T(8,128)}, f32[2,64,512]{2,1,0:T(8,128)S(1)}, u32[]{:S(2)}) copy-start(f32[2,64,512]{2,1,0:T(8,128)S(1)} %fusion.115) | copy-start | bytes 786436
  190.9 25.1 %copy-start.30 = (f32[2,64,512]{2,1,0:T(8,128)S(1)}, f32[2,64,512]{2,1,0:T(8,128)}, u32[]{:S(2)}) copy-start(f32[2,64,512]{2,1,0:T(8,128)} %param.8) | copy-start | bytes 786436
  191.0 6.4 %collective-permute-start.24 = (f32[1,1,64,512]{3,2,1,0:T(8,128)S(1)}, f32[1,1,64,512]{3,2,1,0:T(8,128)S(1)}, u32[]{:S(2)}, u32[]{:S(2)}) collective-permute-start(f32[1,1,64,512]{3,2,1,0:T(8,128)S(1)} %get-tuple-element.48), channel_id=1, source_target_pairs={{0,8},{8,16},{16,24},{1,9},{9,17},{17,25},{2,10},{10,18},{18,26},{... | collective-permute-start | bytes 393224 | tf_op jit(solution)/shard_map/ppermute | solution.py:26
  193.0 6.1 %collective-permute-start.25 = (f32[1,1,64,512]{3,2,1,0:T(8,128)S(1)}, f32[1,1,64,512]{3,2,1,0:T(8,128)S(1)}, u32[]{:S(2)}, u32[]{:S(2)}) collective-permute-start(f32[1,1,64,512]{3,2,1,0:T(8,128)S(1)} %get-tuple-element.49), channel_id=1, source_target_pairs={{8,0},{16,8},{24,16},{9,1},{17,9},{25,17},{10,2},{18,10},{26,18},{... | collective-permute-start | bytes 393224 | tf_op jit(solution)/shard_map/ppermute | solution.py:28
  199.2 3.7 %collective-permute-start.26 = (f32[1,4,1,512]{3,2,1,0:T(1,128)S(1)}, f32[1,4,1,512]{3,2,1,0:T(1,128)S(1)}, u32[]{:S(2)}, u32[]{:S(2)}) collective-permute-start(f32[1,4,1,512]{3,2,1,0:T(1,128)S(1)} %get-tuple-element.34), channel_id=1, source_target_pairs={{0,2},{2,4},{4,6},{1,3},{3,5},{5,7},{8,10},{10,12},{12,14},{9,11},... | collective-permute-start | bytes 24584 | tf_op jit(solution)/shard_map/ppermute | solution.py:26
  201.5 5.5 %collective-permute-start.27 = (f32[1,4,1,512]{3,2,1,0:T(1,128)S(1)}, f32[1,4,1,512]{3,2,1,0:T(1,128)S(1)}, u32[]{:S(2)}, u32[]{:S(2)}) collective-permute-start(f32[1,4,1,512]{3,2,1,0:T(1,128)S(1)} %get-tuple-element.35), channel_id=1, source_target_pairs={{2,0},{4,2},{6,4},{3,1},{5,3},{7,5},{10,8},{12,10},{14,12},{11,9},... | collective-permute-start | bytes 24584 | tf_op jit(solution)/shard_map/ppermute | solution.py:28
  207.2 4.1 %collective-permute-start.28 = (f32[1,4,66,1]{3,2,1,0:T(8,128)S(1)}, f32[1,4,66,1]{3,2,1,0:T(8,128)S(1)}, u32[]{:S(2)}, u32[]{:S(2)}) collective-permute-start(f32[1,4,66,1]{3,2,1,0:T(8,128)S(1)} %get-tuple-element.22), channel_id=1, source_target_pairs={{0,1},{2,3},{4,5},{6,7},{8,9},{10,11},{12,13},{14,15},{16,17},{18,... | collective-permute-start | bytes 3176 | tf_op jit(solution)/shard_map/ppermute | solution.py:26
  208.7 7.0 %collective-permute-start.29 = (f32[1,4,66,1]{3,2,1,0:T(8,128)S(1)}, f32[1,4,66,1]{3,2,1,0:T(8,128)S(1)}, u32[]{:S(2)}, u32[]{:S(2)}) collective-permute-start(f32[1,4,66,1]{3,2,1,0:T(8,128)S(1)} %get-tuple-element.23), channel_id=1, source_target_pairs={{1,0},{3,2},{5,4},{7,6},{9,8},{11,10},{13,12},{15,14},{17,16},{19,... | collective-permute-start | bytes 3176 | tf_op jit(solution)/shard_map/ppermute | solution.py:28
  258.5 28.6 %copy-start.3 = (f32[2,64,512]{2,1,0:T(8,128)S(1)}, f32[2,64,512]{2,1,0:T(8,128)}, u32[]{:S(2)}) copy-start(f32[2,64,512]{2,1,0:T(8,128)} %copy-done.1) | copy-start | bytes 786436
  258.5 28.6 %copy-start.7 = (f32[2,64,512]{2,1,0:T(8,128)S(1)}, f32[2,64,512]{2,1,0:T(8,128)}, u32[]{:S(2)}) copy-start(f32[2,64,512]{2,1,0:T(8,128)} %copy-done.5) | copy-start | bytes 786436
  288.2 29.8 %copy-start.15 = (f32[1,2,64,512]{3,2,1,0:T(8,128)}, f32[1,2,64,512]{3,2,1,0:T(8,128)S(1)}, u32[]{:S(2)}) copy-start(f32[1,2,64,512]{3,2,1,0:T(8,128)S(1)} %fusion.207) | copy-start | bytes 786436
  288.3 7.7 %collective-permute-start.30 = (f32[1,1,64,512]{3,2,1,0:T(8,128)S(1)}, f32[1,1,64,512]{3,2,1,0:T(8,128)S(1)}, u32[]{:S(2)}, u32[]{:S(2)}) collective-permute-start(f32[1,1,64,512]{3,2,1,0:T(8,128)S(1)} %get-tuple-element.46), channel_id=1, source_target_pairs={{0,8},{8,16},{16,24},{1,9},{9,17},{17,25},{2,10},{10,18},{18,26},{... | collective-permute-start | bytes 393224 | tf_op jit(solution)/shard_map/ppermute | solution.py:26
  290.2 6.1 %collective-permute-start.31 = (f32[1,1,64,512]{3,2,1,0:T(8,128)S(1)}, f32[1,1,64,512]{3,2,1,0:T(8,128)S(1)}, u32[]{:S(2)}, u32[]{:S(2)}) collective-permute-start(f32[1,1,64,512]{3,2,1,0:T(8,128)S(1)} %get-tuple-element.47), channel_id=1, source_target_pairs={{8,0},{16,8},{24,16},{9,1},{17,9},{25,17},{10,2},{18,10},{26,18},{... | collective-permute-start | bytes 393224 | tf_op jit(solution)/shard_map/ppermute | solution.py:28
  295.9 22.1 %copy-start.25 = (f32[1,1,64,512]{3,2,1,0:T(8,128)}, f32[1,1,64,512]{3,2,1,0:T(8,128)S(1)}, u32[]{:S(2)}) copy-start(f32[1,1,64,512]{3,2,1,0:T(8,128)S(1)} %collective-permute-done.30) | copy-start | bytes 393220
  296.3 21.7 %copy-start.26 = (f32[1,1,64,512]{3,2,1,0:T(8,128)}, f32[1,1,64,512]{3,2,1,0:T(8,128)S(1)}, u32[]{:S(2)}) copy-start(f32[1,1,64,512]{3,2,1,0:T(8,128)S(1)} %collective-permute-done.31) | copy-start | bytes 393220
  296.4 6.3 %collective-permute-start.32 = (f32[1,4,1,512]{3,2,1,0:T(1,128)S(1)}, f32[1,4,1,512]{3,2,1,0:T(1,128)S(1)}, u32[]{:S(2)}, u32[]{:S(2)}) collective-permute-start(f32[1,4,1,512]{3,2,1,0:T(1,128)S(1)} %get-tuple-element.32), channel_id=1, source_target_pairs={{0,2},{2,4},{4,6},{1,3},{3,5},{5,7},{8,10},{10,12},{12,14},{9,11},... | collective-permute-start | bytes 24584 | tf_op jit(solution)/shard_map/ppermute | solution.py:26
  300.2 5.5 %collective-permute-start.33 = (f32[1,4,1,512]{3,2,1,0:T(1,128)S(1)}, f32[1,4,1,512]{3,2,1,0:T(1,128)S(1)}, u32[]{:S(2)}, u32[]{:S(2)}) collective-permute-start(f32[1,4,1,512]{3,2,1,0:T(1,128)S(1)} %get-tuple-element.33), channel_id=1, source_target_pairs={{2,0},{4,2},{6,4},{3,1},{5,3},{7,5},{10,8},{12,10},{14,12},{11,9},... | collective-permute-start | bytes 24584 | tf_op jit(solution)/shard_map/ppermute | solution.py:28
  306.5 11.5 %collective-permute-start.34 = (f32[1,4,66,1]{3,2,1,0:T(8,128)}, f32[1,4,66,1]{3,2,1,0:T(8,128)S(1)}, u32[]{:S(2)}, u32[]{:S(2)}) collective-permute-start(f32[1,4,66,1]{3,2,1,0:T(8,128)} %get-tuple-element.20), channel_id=1, source_target_pairs={{0,1},{2,3},{4,5},{6,7},{8,9},{10,11},{12,13},{14,15},{16,17},{18,... | collective-permute-start | bytes 3176 | tf_op jit(solution)/shard_map/ppermute | solution.py:26
  310.4 8.7 %collective-permute-start.35 = (f32[1,4,66,1]{3,2,1,0:T(8,128)}, f32[1,4,66,1]{3,2,1,0:T(8,128)}, u32[]{:S(2)}, u32[]{:S(2)}) collective-permute-start(f32[1,4,66,1]{3,2,1,0:T(8,128)} %get-tuple-element.21), channel_id=1, source_target_pairs={{1,0},{3,2},{5,4},{7,6},{9,8},{11,10},{13,12},{15,14},{17,16},{19,... | collective-permute-start | bytes 3176 | tf_op jit(solution)/shard_map/ppermute | solution.py:28
  323.1 11.2 %collective-permute-start.36 = (f32[1,1,64,512]{3,2,1,0:T(8,128)}, f32[1,1,64,512]{3,2,1,0:T(8,128)}, u32[]{:S(2)}, u32[]{:S(2)}) collective-permute-start(f32[1,1,64,512]{3,2,1,0:T(8,128)} %get-tuple-element.44), channel_id=1, source_target_pairs={{0,8},{8,16},{16,24},{1,9},{9,17},{17,25},{2,10},{10,18},{18,26},{... | collective-permute-start | bytes 393224 | tf_op jit(solution)/shard_map/ppermute | solution.py:26
  325.0 9.3 %collective-permute-start.37 = (f32[1,1,64,512]{3,2,1,0:T(8,128)}, f32[1,1,64,512]{3,2,1,0:T(8,128)}, u32[]{:S(2)}, u32[]{:S(2)}) collective-permute-start(f32[1,1,64,512]{3,2,1,0:T(8,128)} %get-tuple-element.45), channel_id=1, source_target_pairs={{8,0},{16,8},{24,16},{9,1},{17,9},{25,17},{10,2},{18,10},{26,18},{... | collective-permute-start | bytes 393224 | tf_op jit(solution)/shard_map/ppermute | solution.py:28
  335.2 6.1 %collective-permute-start.38 = (f32[1,4,1,512]{3,2,1,0:T(1,128)S(1)}, f32[1,4,1,512]{3,2,1,0:T(1,128)S(1)}, u32[]{:S(2)}, u32[]{:S(2)}) collective-permute-start(f32[1,4,1,512]{3,2,1,0:T(1,128)S(1)} %get-tuple-element.30), channel_id=1, source_target_pairs={{0,2},{2,4},{4,6},{1,3},{3,5},{5,7},{8,10},{10,12},{12,14},{9,11},... | collective-permute-start | bytes 24584 | tf_op jit(solution)/shard_map/ppermute | solution.py:26
  337.7 5.5 %collective-permute-start.39 = (f32[1,4,1,512]{3,2,1,0:T(1,128)S(1)}, f32[1,4,1,512]{3,2,1,0:T(1,128)S(1)}, u32[]{:S(2)}, u32[]{:S(2)}) collective-permute-start(f32[1,4,1,512]{3,2,1,0:T(1,128)S(1)} %get-tuple-element.31), channel_id=1, source_target_pairs={{2,0},{4,2},{6,4},{3,1},{5,3},{7,5},{10,8},{12,10},{14,12},{11,9},... | collective-permute-start | bytes 24584 | tf_op jit(solution)/shard_map/ppermute | solution.py:28
  344.2 6.6 %collective-permute-start.40 = (f32[1,4,66,1]{3,2,1,0:T(8,128)S(1)}, f32[1,4,66,1]{3,2,1,0:T(8,128)S(1)}, u32[]{:S(2)}, u32[]{:S(2)}) collective-permute-start(f32[1,4,66,1]{3,2,1,0:T(8,128)S(1)} %get-tuple-element.18), channel_id=1, source_target_pairs={{0,1},{2,3},{4,5},{6,7},{8,9},{10,11},{12,13},{14,15},{16,17},{18,... | collective-permute-start | bytes 3176 | tf_op jit(solution)/shard_map/ppermute | solution.py:26
  348.2 7.0 %collective-permute-start.41 = (f32[1,4,66,1]{3,2,1,0:T(8,128)S(1)}, f32[1,4,66,1]{3,2,1,0:T(8,128)S(1)}, u32[]{:S(2)}, u32[]{:S(2)}) collective-permute-start(f32[1,4,66,1]{3,2,1,0:T(8,128)S(1)} %get-tuple-element.19), channel_id=1, source_target_pairs={{1,0},{3,2},{5,4},{7,6},{9,8},{11,10},{13,12},{15,14},{17,16},{19,... | collective-permute-start | bytes 3176 | tf_op jit(solution)/shard_map/ppermute | solution.py:28
  (41 other events, 395.7 us)
where the time goes:
time: 360 us; the launch traced here: 358 us
  blocking collectives  148 us (41%)
  starting transfers between devices  104 us (29%)
  waiting for transfers between devices  41.1 us (11%)
  other arithmetic  26.6 us (7%)
  matrix products  25.4 us (7%)
  local copies, waits for them, and re-layouts  11.5 us (3%)
    psum x2, blocking collectives, shards(): rhs = lax.psum(local_rhs, ('layer', 'row', 'col')) * (restrict_scale / TILE)  79.9 us
    ppermute x21, starting transfers between devices, padded(): lax.ppermute(tail, axis, [(i, (i + 1) % count) for i in range(ends)])  61.9 us
    psum x8, blocking collectives, shards(): results[section] = lax.psum(placed, 'col')  42.2 us
    ppermute x21, starting transfers between devices, padded(): lax.ppermute(head, axis, [((i + 1) % count, i) for i in range(ends)])  42 us
    ppermute x21, waiting for transfers between devices, padded(): lax.ppermute(head, axis, [((i + 1) % count, i) for i in range(ends)])  35.7 us
    all_gather x6, blocking collectives, shards(): full = lax.all_gather(piece, 'col', axis=0, tiled=True)  25.4 us
    dot_general x8, matrix products, shards(): jnp.dot(pivots[section], forward[section], precision=highest)  10.7 us
  transfers between devices with their start and end apart: 42, of which 16 were waited for; matrix products, arithmetic and copies ran while one was open for 5% of the time, Pallas kernels for 0%

commit v1 on v0

--- a/solution.py
+++ b/solution.py
@@ -114,7 +114,9 @@
         plane = jnp.sum(resid, axis=0)
         row_sums = jnp.dot(row_select, plane, precision=highest)
         local_rhs = jnp.sum(row_sums * col_select, axis=1).reshape(NPANEL, PANEL)
-        rhs = lax.psum(local_rhs, ("layer", "row", "col")) * (restrict_scale / TILE)
+        rhs = jnp.sum(lax.all_gather(local_rhs, ("layer", "row", "col")), axis=0) * (
+            restrict_scale / TILE
+        )
         full = rhs[0]
         forward = [full]
         for section in range(1, NPANEL):

time: 360 us -> 403 us (1.12)
  blocking collectives: 148 us -> 199 us
  starting transfers between devices: 104 us -> 95.5 us
    all_gather x0 -> x2, blocking collectives: none -> 131 us  [shards(): lax.all_gather(local_rhs, ('layer', 'row', 'col'))]
    psum x2 -> x0, blocking collectives: 79.9 us -> none  [shards(): rhs = lax.psum(local_rhs, ('layer', 'row', 'col')) * (restrict_scale / TILE)]
    ppermute x21, starting transfers between devices: 61.9 us -> 53.3 us  [padded(): lax.ppermute(tail, axis, [(i, (i + 1) % count) for i in range(ends)])]
  transfers between devices with their start and end apart: 42 -> 42, of which waited for: 16 -> 16; matrix products, arithmetic and copies ran while one was open for 5% -> 4% of each run, Pallas kernels for 0% -> 0%
where the time goes in v1:
time: 403 us; the launch traced here: 402 us
  blocking collectives  199 us (49%)
  starting transfers between devices  95.5 us (24%)
  waiting for transfers between devices  41.1 us (10%)
  other arithmetic  26.7 us (7%)
  matrix products  25.4 us (6%)
  local copies, waits for them, and re-layouts  11.5 us (3%)
    all_gather x2, blocking collectives, shards(): lax.all_gather(local_rhs, ('layer', 'row', 'col'))  131 us
    ppermute x21, starting transfers between devices, padded(): lax.ppermute(tail, axis, [(i, (i + 1) % count) for i in range(ends)])  53.3 us
    ppermute x21, starting transfers between devices, padded(): lax.ppermute(head, axis, [((i + 1) % count, i) for i in range(ends)])  42.2 us
    psum x8, blocking collectives, shards(): results[section] = lax.psum(placed, 'col')  42.1 us
    ppermute x21, waiting for transfers between devices, padded(): lax.ppermute(head, axis, [((i + 1) % count, i) for i in range(ends)])  35.7 us
    all_gather x6, blocking collectives, shards(): full = lax.all_gather(piece, 'col', axis=0, tiled=True)  25.7 us
    dot_general x8, matrix products, shards(): jnp.dot(pivots[section], forward[section], precision=highest)  10.7 us
  transfers between devices with their start and end apart: 42, of which 16 were waited for; matrix products, arithmetic and copies ran while one was open for 4% of the time, Pallas kernels for 0%

profile of v1, /device:TPU:2, one launch (start us, length us, event | category | flops | bytes accessed | tf_op | source)
XLA Modules:
  0.0 401.6 jit_solution(6283689891811974102)
XLA Ops:
  0.7 2.1 collective-permute-start.7
  2.7 2.4 collective-permute-start.6
  7.2 1.9 collective-permute-start
  9.2 3.6 collective-permute-start.1
  13.1 3.5 collective-permute-start.8
  17.9 4.5 %collective-permute-start.2 = (f32[2,4,1,512]{3,2,1,0:T(1,128)S(1)}, f32[2,4,1,512]{3,2,1,0:T(1,128)S(1)}, u32[]{:S(2)}, u32[]{:S(2)}) collective-permute-start(f32[2,4,1,512]{3,2,1,0:T(1,128)S(1)} %get-tuple-element.16), channel_id=1, source_target_pairs={{0,2},{2,4},{4,6},{1,3},{3,5},{5,7},{8,10},{10,12},{12,14},{9,11},... | collective-permute-start | bytes 49160 | tf_op jit(solution)/shard_map/ppermute | solution.py:26
  23.9 3.4 collective-permute-start.10
  28.8 4.6 %collective-permute-start.4 = (f32[2,4,66,1]{3,2,1,0:T(8,128)S(1)}, f32[2,4,66,1]{3,2,1,0:T(8,128)S(1)}, u32[]{:S(2)}, u32[]{:S(2)}) collective-permute-start(f32[2,4,66,1]{3,2,1,0:T(8,128)S(1)} %get-tuple-element.14), channel_id=1, source_target_pairs={{0,1},{2,3},{4,5},{6,7},{8,9},{10,11},{12,13},{14,15},{16,17},{18,... | collective-permute-start | bytes 6344 | tf_op jit(solution)/shard_map/ppermute | solution.py:26
  35.1 2.5 collective-permute-done.4
  37.6 4.4 %collective-permute-done.5 = f32[2,4,66,1]{3,2,1,0:T(8,128)S(1)} collective-permute-done((f32[2,4,66,1]{3,2,1,0:T(8,128)S(1)}, f32[2,4,66,1]{3,2,1,0:T(8,128)S(1)}, u32[]{:S(2)}, u32[]{:S(2)}) %collective-permute-start.5) | collective-permute-done | bytes 2144 | tf_op jit(solution)/shard_map/ppermute | solution.py:28
  43.8 1.7 fusion.211
  45.5 2.6 fusion.4
  48.1 66.8 %all_gather.24 = f32[32,4,512]{2,1,0:T(4,128)S(1)} all-gather(f32[1,4,512]{2,1,0:T(4,128)S(1)} %all_gather_reshape.6), channel_id=1, replica_groups=mesh['layer'=4,'row'=4,'col'=2] {'layer','row','col'}, dimensions={0}, use_global_device_ids=true | all-gather | bytes 270336 | tf_op jit(solution)/shard_map/all_gather | solution.py:117
  115.5 2.2 fusion.56
  117.7 4.2 %all-gather = f32[2,1,256]{2,1,0:T(1,128)S(1)} all-gather(f32[1,1,256]{2,1,0:T(1,128)S(1)} %bitcast.242), channel_id=1, replica_groups=mesh['layer'=4,'row'=4,'col'=2] {'col'}, dimensions={0}, use_global_device_ids=true | all-gather | bytes 3072 | tf_op jit(solution)/shard_map/all_gather | solution.py:126
  122.5 4.2 %all-gather.1 = f32[2,1,256]{2,1,0:T(1,128)S(1)} all-gather(f32[1,1,256]{2,1,0:T(1,128)S(1)} %bitcast.243), channel_id=1, replica_groups=mesh['layer'=4,'row'=4,'col'=2] {'col'}, dimensions={0}, use_global_device_ids=true | all-gather | bytes 3072 | tf_op jit(solution)/shard_map/all_gather | solution.py:126
  127.8 4.2 %all-gather.2 = f32[2,1,256]{2,1,0:T(1,128)S(1)} all-gather(f32[1,1,256]{2,1,0:T(1,128)S(1)} %bitcast.244), channel_id=1, replica_groups=mesh['layer'=4,'row'=4,'col'=2] {'col'}, dimensions={0}, use_global_device_ids=true | all-gather | bytes 3072 | tf_op jit(solution)/shard_map/all_gather | solution.py:126
  132.8 4.9 %psum.56 = f32[512]{0:T(512)S(1)} all-reduce(f32[512]{0:T(512)S(1)} %dynamic_update_slice.27), channel_id=1, replica_groups=mesh['layer'=4,'row'=4,'col'=2] {'col'}, use_global_device_ids=true, to_apply=%region_3.4 | all-reduce | flops 512 | bytes 4096 | tf_op jit(solution)/shard_map/psum | solution.py:140
  138.3 4.9 %psum.57 = f32[512]{0:T(512)S(1)} all-reduce(f32[512]{0:T(512)S(1)} %sub.193), channel_id=1, replica_groups=mesh['layer'=4,'row'=4,'col'=2] {'col'}, use_global_device_ids=true, to_apply=%region_4.5 | all-reduce | flops 512 | bytes 4096 | tf_op jit(solution)/shard_map/psum | solution.py:140
  145.0 1.9 collective-permute-start.12
  146.9 3.6 collective-permute-start.13
  150.6 2.1 fusion.44
  156.9 3.1 collective-permute-done.15
  160.7 2.1 collective-permute-start.16
  164.2 6.2 %psum.58 = f32[512]{0:T(512)S(1)} all-reduce(f32[512]{0:T(512)S(1)} %sub.194), channel_id=1, replica_groups=mesh['layer'=4,'row'=4,'col'=2] {'col'}, use_global_device_ids=true, to_apply=%region_5.6 | all-reduce | flops 512 | bytes 4096 | tf_op jit(solution)/shard_map/psum | solution.py:140
  174.6 1.7 fusion.196
  177.7 1.9 collective-permute-start.18
  179.6 3.8 collective-permute-start.19
  183.8 4.9 %psum.59 = f32[1,512]{1,0:T(1,128)S(1)} all-reduce(f32[1,512]{1,0:T(1,128)S(1)} %bitcast.217), channel_id=1, replica_groups=mesh['layer'=4,'row'=4,'col'=2] {'col'}, use_global_device_ids=true, to_apply=%region_6.7 | all-reduce | flops 512 | bytes 4096 | tf_op jit(solution)/shard_map/psum | solution.py:140
  189.7 1.6 collective-permute-start.20
  192.7 4.2 %collective-permute-done.21 = f32[1,4,1,512]{3,2,1,0:T(1,128)S(1)} collective-permute-done((f32[1,4,1,512]{3,2,1,0:T(1,128)S(1)}, f32[1,4,1,512]{3,2,1,0:T(1,128)S(1)}, u32[]{:S(2)}, u32[]{:S(2)}) %collective-permute-start.21) | collective-permute-done | bytes 8224 | tf_op jit(solution)/shard_map/ppermute | solution.py:28
  197.9 4.0 collective-permute-start.22
  203.2 2.2 fusion.12
  205.4 3.5 collective-permute-done.23
  211.3 2.1 collective-permute-start.24
  213.3 3.6 collective-permute-start.25
  217.7 1.8 collective-permute-done.25
  219.5 1.9 collective-permute-start.26
  222.8 4.2 %collective-permute-done.27 = f32[1,4,1,512]{3,2,1,0:T(1,128)S(1)} collective-permute-done((f32[1,4,1,512]{3,2,1,0:T(1,128)S(1)}, f32[1,4,1,512]{3,2,1,0:T(1,128)S(1)}, u32[]{:S(2)}, u32[]{:S(2)}) %collective-permute-start.27) | collective-permute-done | bytes 8224 | tf_op jit(solution)/shard_map/ppermute | solution.py:28
  231.2 4.4 %collective-permute-done.29 = f32[1,4,66,1]{3,2,1,0:T(8,128)S(1)} collective-permute-done((f32[1,4,66,1]{3,2,1,0:T(8,128)S(1)}, f32[1,4,66,1]{3,2,1,0:T(8,128)S(1)}, u32[]{:S(2)}, u32[]{:S(2)}) %collective-permute-start.29) | collective-permute-done | bytes 1088 | tf_op jit(solution)/shard_map/ppermute | solution.py:28
  237.1 2.5 fusion.5
  239.7 64.7 %all_gather.28 = f32[32,4,512]{2,1,0:T(4,128)S(1)} all-gather(f32[1,4,512]{2,1,0:T(4,128)S(1)} %all_gather_reshape.7), channel_id=1, replica_groups=mesh['layer'=4,'row'=4,'col'=2] {'layer','row','col'}, dimensions={0}, use_global_device_ids=true | all-gather | bytes 270336 | tf_op jit(solution)/shard_map/all_gather | solution.py:117
  305.0 2.2 fusion.54
  307.3 4.5 %all-gather.3 = f32[2,1,256]{2,1,0:T(1,128)S(1)} all-gather(f32[1,1,256]{2,1,0:T(1,128)S(1)} %bitcast.245), channel_id=1, replica_groups=mesh['layer'=4,'row'=4,'col'=2] {'col'}, dimensions={0}, use_global_device_ids=true | all-gather | bytes 3072 | tf_op jit(solution)/shard_map/all_gather | solution.py:126
  312.3 4.2 %all-gather.4 = f32[2,1,256]{2,1,0:T(1,128)S(1)} all-gather(f32[1,1,256]{2,1,0:T(1,128)S(1)} %bitcast.246), channel_id=1, replica_groups=mesh['layer'=4,'row'=4,'col'=2] {'col'}, dimensions={0}, use_global_device_ids=true | all-gather | bytes 3072 | tf_op jit(solution)/shard_map/all_gather | solution.py:126
  317.6 4.2 %all-gather.5 = f32[2,1,256]{2,1,0:T(1,128)S(1)} all-gather(f32[1,1,256]{2,1,0:T(1,128)S(1)} %bitcast.247), channel_id=1, replica_groups=mesh['layer'=4,'row'=4,'col'=2] {'col'}, dimensions={0}, use_global_device_ids=true | all-gather | bytes 3072 | tf_op jit(solution)/shard_map/all_gather | solution.py:126
  322.6 4.9 %psum.60 = f32[512]{0:T(512)S(1)} all-reduce(f32[512]{0:T(512)S(1)} %dynamic_update_slice.31), channel_id=1, replica_groups=mesh['layer'=4,'row'=4,'col'=2] {'col'}, use_global_device_ids=true, to_apply=%region_10.11 | all-reduce | flops 512 | bytes 4096 | tf_op jit(solution)/shard_map/psum | solution.py:140
  328.2 4.9 %psum.61 = f32[512]{0:T(512)S(1)} all-reduce(f32[512]{0:T(512)S(1)} %sub.220), channel_id=1, replica_groups=mesh['layer'=4,'row'=4,'col'=2] {'col'}, use_global_device_ids=true, to_apply=%region_11.12 | all-reduce | flops 512 | bytes 4096 | tf_op jit(solution)/shard_map/psum | solution.py:140
  334.8 1.9 collective-permute-start.30
  336.8 3.6 collective-permute-start.31
  340.4 2.1 fusion.42
  346.7 3.1 collective-permute-done.33
  350.6 3.9 collective-permute-start.34
  355.8 6.4 %psum.62 = f32[512]{0:T(512)S(1)} all-reduce(f32[512]{0:T(512)S(1)} %sub.221), channel_id=1, replica_groups=mesh['layer'=4,'row'=4,'col'=2] {'col'}, use_global_device_ids=true, to_apply=%region_12.13 | all-reduce | flops 512 | bytes 4096 | tf_op jit(solution)/shard_map/psum | solution.py:140
  365.0 1.7 fusion.194
  367.4 1.9 collective-permute-start.36
  369.3 3.6 collective-permute-start.37
  373.6 4.9 %psum.63 = f32[1,512]{1,0:T(1,128)S(1)} all-reduce(f32[1,512]{1,0:T(1,128)S(1)} %bitcast.218), channel_id=1, replica_groups=mesh['layer'=4,'row'=4,'col'=2] {'col'}, use_global_device_ids=true, to_apply=%region_13.14 | all-reduce | flops 512 | bytes 4096 | tf_op jit(solution)/shard_map/psum | solution.py:140
  379.4 1.6 collective-permute-start.38
  382.4 2.2 fusion.15
  384.7 2.0 collective-permute-done.39
  387.6 4.0 collective-permute-start.40
  394.2 4.4 %collective-permute-done.41 = f32[1,4,66,1]{3,2,1,0:T(8,128)S(1)} collective-permute-done((f32[1,4,66,1]{3,2,1,0:T(8,128)S(1)}, f32[1,4,66,1]{3,2,1,0:T(8,128)S(1)}, u32[]{:S(2)}, u32[]{:S(2)}) %collective-permute-start.41) | collective-permute-done | bytes 1088 | tf_op jit(solution)/shard_map/ppermute | solution.py:28
  399.9 1.6 fusion.142
  (283 shorter events, 64.7 us)
Async XLA Ops:
  0.7 12.3 %collective-permute-start.7 = (f32[1,1,64,512]{3,2,1,0:T(8,128)S(1)}, f32[1,1,64,512]{3,2,1,0:T(8,128)S(1)}, u32[]{:S(2)}, u32[]{:S(2)}) collective-permute-start(f32[1,1,64,512]{3,2,1,0:T(8,128)S(1)} %broadcast.185), channel_id=1, source_target_pairs={{8,0},{16,8},{24,16},{9,1},{17,9},{25,17},{10,2},{18,10},{26,18},{... | collective-permute-start | bytes 393224 | tf_op jit(solution)/shard_map/ppermute | solution.py:28
  2.7 10.3 %collective-permute-start.6 = (f32[1,1,64,512]{3,2,1,0:T(8,128)S(1)}, f32[1,1,64,512]{3,2,1,0:T(8,128)S(1)}, u32[]{:S(2)}, u32[]{:S(2)}) collective-permute-start(f32[1,1,64,512]{3,2,1,0:T(8,128)S(1)} %broadcast.185), channel_id=1, source_target_pairs={{0,8},{8,16},{16,24},{1,9},{9,17},{17,25},{2,10},{10,18},{18,26},{... | collective-permute-start | bytes 393224 | tf_op jit(solution)/shard_map/ppermute | solution.py:26
  7.2 10.6 %collective-permute-start = (f32[2,1,64,512]{3,2,1,0:T(8,128)S(1)}, f32[2,1,64,512]{3,2,1,0:T(8,128)S(1)}, u32[]{:S(2)}, u32[]{:S(2)}) collective-permute-start(f32[2,1,64,512]{3,2,1,0:T(8,128)S(1)} %get-tuple-element.40), channel_id=1, source_target_pairs={{0,8},{8,16},{16,24},{1,9},{9,17},{17,25},{2,10},{10,18},{18,26},{... | collective-permute-start | bytes 786440 | tf_op jit(solution)/shard_map/ppermute | solution.py:26
  9.2 8.7 %collective-permute-start.1 = (f32[2,1,64,512]{3,2,1,0:T(8,128)S(1)}, f32[2,1,64,512]{3,2,1,0:T(8,128)S(1)}, u32[]{:S(2)}, u32[]{:S(2)}) collective-permute-start(f32[2,1,64,512]{3,2,1,0:T(8,128)S(1)} %get-tuple-element.41), channel_id=1, source_target_pairs={{8,0},{16,8},{24,16},{9,1},{17,9},{25,17},{10,2},{18,10},{26,18},{... | collective-permute-start | bytes 786440 | tf_op jit(solution)/shard_map/ppermute | solution.py:28
  12.9 32.6 %copy-start.46 = (s32[2048]{0:T(1024)}, s32[2048]{0:T(1024)S(1)}, u32[]{:S(2)}) copy-start(s32[2048]{0:T(1024)S(1)} %get-tuple-element.60) | copy-start | bytes 24580
  12.9 32.6 %copy-start.49 = (s32[2048]{0:T(1024)}, s32[2048]{0:T(1024)S(1)}, u32[]{:S(2)}) copy-start(s32[2048]{0:T(1024)S(1)} %get-tuple-element.61) | copy-start | bytes 24580
  12.9 32.6 %copy-start.60 = (s32[64]{0:T(128)}, s32[64]{0:T(128)S(1)}, u32[]{:S(2)}) copy-start(s32[64]{0:T(128)S(1)} %and_select_fusion) | copy-start | bytes 772
  13.0 32.5 %copy-start.57 = (s32[512]{0:T(512)}, s32[512]{0:T(512)S(1)}, u32[]{:S(2)}) copy-start(s32[512]{0:T(512)S(1)} %add_select_fusion.2) | copy-start | bytes 6148
  13.1 10.7 %collective-permute-start.8 = (f32[1,4,1,512]{3,2,1,0:T(1,128)S(1)}, f32[1,4,1,512]{3,2,1,0:T(1,128)S(1)}, u32[]{:S(2)}, u32[]{:S(2)}) collective-permute-start(f32[1,4,1,512]{3,2,1,0:T(1,128)S(1)} %get-tuple-element.42), channel_id=1, source_target_pairs={{0,2},{2,4},{4,6},{1,3},{3,5},{5,7},{8,10},{10,12},{12,14},{9,11},... | collective-permute-start | bytes 24584 | tf_op jit(solution)/shard_map/ppermute | solution.py:26
  16.5 7.2 %collective-permute-start.9 = (f32[1,4,1,512]{3,2,1,0:T(1,128)S(1)}, f32[1,4,1,512]{3,2,1,0:T(1,128)S(1)}, u32[]{:S(2)}, u32[]{:S(2)}) collective-permute-start(f32[1,4,1,512]{3,2,1,0:T(1,128)S(1)} %get-tuple-element.43), channel_id=1, source_target_pairs={{2,0},{4,2},{6,4},{3,1},{5,3},{7,5},{10,8},{12,10},{14,12},{11,9},... | collective-permute-start | bytes 24584 | tf_op jit(solution)/shard_map/ppermute | solution.py:28
  17.9 10.7 %collective-permute-start.2 = (f32[2,4,1,512]{3,2,1,0:T(1,128)S(1)}, f32[2,4,1,512]{3,2,1,0:T(1,128)S(1)}, u32[]{:S(2)}, u32[]{:S(2)}) collective-permute-start(f32[2,4,1,512]{3,2,1,0:T(1,128)S(1)} %get-tuple-element.16), channel_id=1, source_target_pairs={{0,2},{2,4},{4,6},{1,3},{3,5},{5,7},{8,10},{10,12},{12,14},{9,11},... | collective-permute-start | bytes 49160 | tf_op jit(solution)/shard_map/ppermute | solution.py:26
  22.5 6.2 %collective-permute-start.3 = (f32[2,4,1,512]{3,2,1,0:T(1,128)S(1)}, f32[2,4,1,512]{3,2,1,0:T(1,128)S(1)}, u32[]{:S(2)}, u32[]{:S(2)}) collective-permute-start(f32[2,4,1,512]{3,2,1,0:T(1,128)S(1)} %get-tuple-element.17), channel_id=1, source_target_pairs={{2,0},{4,2},{6,4},{3,1},{5,3},{7,5},{10,8},{12,10},{14,12},{11,9},... | collective-permute-start | bytes 49160 | tf_op jit(solution)/shard_map/ppermute | solution.py:28
  23.9 10.8 %collective-permute-start.10 = (f32[1,4,66,1]{3,2,1,0:T(8,128)S(1)}, f32[1,4,66,1]{3,2,1,0:T(8,128)S(1)}, u32[]{:S(2)}, u32[]{:S(2)}) collective-permute-start(f32[1,4,66,1]{3,2,1,0:T(8,128)S(1)} %get-tuple-element.28), channel_id=1, source_target_pairs={{0,1},{2,3},{4,5},{6,7},{8,9},{10,11},{12,13},{14,15},{16,17},{18,... | collective-permute-start | bytes 3176 | tf_op jit(solution)/shard_map/ppermute | solution.py:26
  27.4 7.4 %collective-permute-start.11 = (f32[1,4,66,1]{3,2,1,0:T(8,128)S(1)}, f32[1,4,66,1]{3,2,1,0:T(8,128)S(1)}, u32[]{:S(2)}, u32[]{:S(2)}) collective-permute-start(f32[1,4,66,1]{3,2,1,0:T(8,128)S(1)} %get-tuple-element.29), channel_id=1, source_target_pairs={{1,0},{3,2},{5,4},{7,6},{9,8},{11,10},{13,12},{15,14},{17,16},{19,... | collective-permute-start | bytes 3176 | tf_op jit(solution)/shard_map/ppermute | solution.py:28
  28.8 8.8 %collective-permute-start.4 = (f32[2,4,66,1]{3,2,1,0:T(8,128)S(1)}, f32[2,4,66,1]{3,2,1,0:T(8,128)S(1)}, u32[]{:S(2)}, u32[]{:S(2)}) collective-permute-start(f32[2,4,66,1]{3,2,1,0:T(8,128)S(1)} %get-tuple-element.14), channel_id=1, source_target_pairs={{0,1},{2,3},{4,5},{6,7},{8,9},{10,11},{12,13},{14,15},{16,17},{18,... | collective-permute-start | bytes 6344 | tf_op jit(solution)/shard_map/ppermute | solution.py:26
  33.4 8.6 %collective-permute-start.5 = (f32[2,4,66,1]{3,2,1,0:T(8,128)S(1)}, f32[2,4,66,1]{3,2,1,0:T(8,128)S(1)}, u32[]{:S(2)}, u32[]{:S(2)}) collective-permute-start(f32[2,4,66,1]{3,2,1,0:T(8,128)S(1)} %get-tuple-element.15), channel_id=1, source_target_pairs={{1,0},{3,2},{5,4},{7,6},{9,8},{11,10},{13,12},{15,14},{17,16},{19,... | collective-permute-start | bytes 6344 | tf_op jit(solution)/shard_map/ppermute | solution.py:28
  45.5 98.3 %copy-start.1 = (f32[2,64,512]{2,1,0:T(8,128)}, f32[2,64,512]{2,1,0:T(8,128)S(1)}, u32[]{:S(2)}) copy-start(f32[2,64,512]{2,1,0:T(8,128)S(1)} %get-tuple-element.10) | copy-start | bytes 786436
  45.5 98.3 %copy-start.5 = (f32[2,64,512]{2,1,0:T(8,128)}, f32[2,64,512]{2,1,0:T(8,128)S(1)}, u32[]{:S(2)}) copy-start(f32[2,64,512]{2,1,0:T(8,128)S(1)} %get-tuple-element.11) | copy-start | bytes 786436
  45.5 69.4 %copy-start = (f32[3,256,512]{2,1,0:T(8,128)S(1)}, f32[3,256,512]{2,1,0:T(8,128)}, u32[]{:S(2)}) copy-start(f32[3,256,512]{2,1,0:T(8,128)} %param.15) | copy-start | bytes 4718596
  145.0 26.8 %copy-start.14 = (f32[1,2,64,512]{3,2,1,0:T(8,128)}, f32[1,2,64,512]{3,2,1,0:T(8,128)S(1)}, u32[]{:S(2)}) copy-start(f32[1,2,64,512]{3,2,1,0:T(8,128)S(1)} %fusion.208) | copy-start | bytes 786436
  145.0 7.7 %collective-permute-start.12 = (f32[1,1,64,512]{3,2,1,0:T(8,128)S(1)}, f32[1,1,64,512]{3,2,1,0:T(8,128)S(1)}, u32[]{:S(2)}, u32[]{:S(2)}) collective-permute-start(f32[1,1,64,512]{3,2,1,0:T(8,128)S(1)} %get-tuple-element.52), channel_id=1, source_target_pairs={{0,8},{8,16},{16,24},{1,9},{9,17},{17,25},{2,10},{10,18},{18,26},{... | collective-permute-start | bytes 393224 | tf_op jit(solution)/shard_map/ppermute | solution.py:26
  146.9 6.1 %collective-permute-start.13 = (f32[1,1,64,512]{3,2,1,0:T(8,128)S(1)}, f32[1,1,64,512]{3,2,1,0:T(8,128)S(1)}, u32[]{:S(2)}, u32[]{:S(2)}) collective-permute-start(f32[1,1,64,512]{3,2,1,0:T(8,128)S(1)} %get-tuple-element.53), channel_id=1, source_target_pairs={{8,0},{16,8},{24,16},{9,1},{17,9},{25,17},{10,2},{18,10},{26,18},{... | collective-permute-start | bytes 393224 | tf_op jit(solution)/shard_map/ppermute | solution.py:28
  152.7 19.1 %copy-start.23 = (f32[1,1,64,512]{3,2,1,0:T(8,128)}, f32[1,1,64,512]{3,2,1,0:T(8,128)S(1)}, u32[]{:S(2)}) copy-start(f32[1,1,64,512]{3,2,1,0:T(8,128)S(1)} %collective-permute-done.12) | copy-start | bytes 393220
  153.1 3.8 collective-permute-start.14
  154.4 5.5 %collective-permute-start.15 = (f32[1,4,1,512]{3,2,1,0:T(1,128)S(1)}, f32[1,4,1,512]{3,2,1,0:T(1,128)S(1)}, u32[]{:S(2)}, u32[]{:S(2)}) collective-permute-start(f32[1,4,1,512]{3,2,1,0:T(1,128)S(1)} %get-tuple-element.39), channel_id=1, source_target_pairs={{2,0},{4,2},{6,4},{3,1},{5,3},{7,5},{10,8},{12,10},{14,12},{11,9},... | collective-permute-start | bytes 24584 | tf_op jit(solution)/shard_map/ppermute | solution.py:28
  160.7 11.1 %collective-permute-start.16 = (f32[1,4,66,1]{3,2,1,0:T(8,128)}, f32[1,4,66,1]{3,2,1,0:T(8,128)S(1)}, u32[]{:S(2)}, u32[]{:S(2)}) collective-permute-start(f32[1,4,66,1]{3,2,1,0:T(8,128)} %get-tuple-element.26), channel_id=1, source_target_pairs={{0,1},{2,3},{4,5},{6,7},{8,9},{10,11},{12,13},{14,15},{16,17},{18,... | collective-permute-start | bytes 3176 | tf_op jit(solution)/shard_map/ppermute | solution.py:26
  162.9 10.2 %collective-permute-start.17 = (f32[1,4,66,1]{3,2,1,0:T(8,128)}, f32[1,4,66,1]{3,2,1,0:T(8,128)}, u32[]{:S(2)}, u32[]{:S(2)}) collective-permute-start(f32[1,4,66,1]{3,2,1,0:T(8,128)} %get-tuple-element.27), channel_id=1, source_target_pairs={{1,0},{3,2},{5,4},{7,6},{9,8},{11,10},{13,12},{15,14},{17,16},{19,... | collective-permute-start | bytes 3176 | tf_op jit(solution)/shard_map/ppermute | solution.py:28
  176.9 26.2 %copy-start.47 = (s32[2048]{0:T(1024)S(1)}, s32[2048]{0:T(1024)}, u32[]{:S(2)}) copy-start(s32[2048]{0:T(1024)} %copy-done.46) | copy-start | bytes 24580
  177.0 26.2 %copy-start.50 = (s32[2048]{0:T(1024)S(1)}, s32[2048]{0:T(1024)}, u32[]{:S(2)}) copy-start(s32[2048]{0:T(1024)} %copy-done.49) | copy-start | bytes 24580
  177.0 26.2 %copy-start.58 = (s32[512]{0:T(512)S(1)}, s32[512]{0:T(512)}, u32[]{:S(2)}) copy-start(s32[512]{0:T(512)} %copy-done.57) | copy-start | bytes 6148
  177.0 26.2 %copy-start.61 = (s32[64]{0:T(128)S(1)}, s32[64]{0:T(128)}, u32[]{:S(2)}) copy-start(s32[64]{0:T(128)} %copy-done.60) | copy-start | bytes 772
  177.7 11.1 %collective-permute-start.18 = (f32[1,1,64,512]{3,2,1,0:T(8,128)}, f32[1,1,64,512]{3,2,1,0:T(8,128)}, u32[]{:S(2)}, u32[]{:S(2)}) collective-permute-start(f32[1,1,64,512]{3,2,1,0:T(8,128)} %get-tuple-element.50), channel_id=1, source_target_pairs={{0,8},{8,16},{16,24},{1,9},{9,17},{17,25},{2,10},{10,18},{18,26},{... | collective-permute-start | bytes 393224 | tf_op jit(solution)/shard_map/ppermute | solution.py:26
  179.6 9.2 %collective-permute-start.19 = (f32[1,1,64,512]{3,2,1,0:T(8,128)}, f32[1,1,64,512]{3,2,1,0:T(8,128)}, u32[]{:S(2)}, u32[]{:S(2)}) collective-permute-start(f32[1,1,64,512]{3,2,1,0:T(8,128)} %get-tuple-element.51), channel_id=1, source_target_pairs={{8,0},{16,8},{24,16},{9,1},{17,9},{25,17},{10,2},{18,10},{26,18},{... | collective-permute-start | bytes 393224 | tf_op jit(solution)/shard_map/ppermute | solution.py:28
  188.8 20.1 %copy-start.20 = (f32[1,2,64,512]{3,2,1,0:T(8,128)S(1)}, f32[1,2,64,512]{3,2,1,0:T(8,128)}, u32[]{:S(2)}) copy-start(f32[1,2,64,512]{3,2,1,0:T(8,128)} %copy-done.19) | copy-start | bytes 786436
  189.7 3.0 collective-permute-start.20
  191.3 5.5 %collective-permute-start.21 = (f32[1,4,1,512]{3,2,1,0:T(1,128)S(1)}, f32[1,4,1,512]{3,2,1,0:T(1,128)S(1)}, u32[]{:S(2)}, u32[]{:S(2)}) collective-permute-start(f32[1,4,1,512]{3,2,1,0:T(1,128)S(1)} %get-tuple-element.37), channel_id=1, source_target_pairs={{2,0},{4,2},{6,4},{3,1},{5,3},{7,5},{10,8},{12,10},{14,12},{11,9},... | collective-permute-start | bytes 24584 | tf_op jit(solution)/shard_map/ppermute | solution.py:28
  197.9 7.5 %collective-permute-start.22 = (f32[1,4,66,1]{3,2,1,0:T(8,128)S(1)}, f32[1,4,66,1]{3,2,1,0:T(8,128)S(1)}, u32[]{:S(2)}, u32[]{:S(2)}) collective-permute-start(f32[1,4,66,1]{3,2,1,0:T(8,128)S(1)} %get-tuple-element.24), channel_id=1, source_target_pairs={{0,1},{2,3},{4,5},{6,7},{8,9},{10,11},{12,13},{14,15},{16,17},{18,... | collective-permute-start | bytes 3176 | tf_op jit(solution)/shard_map/ppermute | solution.py:26
  201.9 7.0 %collective-permute-start.23 = (f32[1,4,66,1]{3,2,1,0:T(8,128)S(1)}, f32[1,4,66,1]{3,2,1,0:T(8,128)S(1)}, u32[]{:S(2)}, u32[]{:S(2)}) collective-permute-start(f32[1,4,66,1]{3,2,1,0:T(8,128)S(1)} %get-tuple-element.25), channel_id=1, source_target_pairs={{1,0},{3,2},{5,4},{7,6},{9,8},{11,10},{13,12},{15,14},{17,16},{19,... | collective-permute-start | bytes 3176 | tf_op jit(solution)/shard_map/ppermute | solution.py:28
  211.2 24.7 %copy-start.9 = (f32[2,64,512]{2,1,0:T(8,128)}, f32[2,64,512]{2,1,0:T(8,128)S(1)}, u32[]{:S(2)}) copy-start(f32[2,64,512]{2,1,0:T(8,128)S(1)} %fusion.115) | copy-start | bytes 786436
  211.3 24.7 %copy-start.30 = (f32[2,64,512]{2,1,0:T(8,128)S(1)}, f32[2,64,512]{2,1,0:T(8,128)}, u32[]{:S(2)}) copy-start(f32[2,64,512]{2,1,0:T(8,128)} %param.8) | copy-start | bytes 786436
  211.3 6.4 %collective-permute-start.24 = (f32[1,1,64,512]{3,2,1,0:T(8,128)S(1)}, f32[1,1,64,512]{3,2,1,0:T(8,128)S(1)}, u32[]{:S(2)}, u32[]{:S(2)}) collective-permute-start(f32[1,1,64,512]{3,2,1,0:T(8,128)S(1)} %get-tuple-element.48), channel_id=1, source_target_pairs={{0,8},{8,16},{16,24},{1,9},{9,17},{17,25},{2,10},{10,18},{18,26},{... | collective-permute-start | bytes 393224 | tf_op jit(solution)/shard_map/ppermute | solution.py:26
  213.3 6.1 %collective-permute-start.25 = (f32[1,1,64,512]{3,2,1,0:T(8,128)S(1)}, f32[1,1,64,512]{3,2,1,0:T(8,128)S(1)}, u32[]{:S(2)}, u32[]{:S(2)}) collective-permute-start(f32[1,1,64,512]{3,2,1,0:T(8,128)S(1)} %get-tuple-element.49), channel_id=1, source_target_pairs={{8,0},{16,8},{24,16},{9,1},{17,9},{25,17},{10,2},{18,10},{26,18},{... | collective-permute-start | bytes 393224 | tf_op jit(solution)/shard_map/ppermute | solution.py:28
  219.5 3.3 collective-permute-start.26
  221.4 5.5 %collective-permute-start.27 = (f32[1,4,1,512]{3,2,1,0:T(1,128)S(1)}, f32[1,4,1,512]{3,2,1,0:T(1,128)S(1)}, u32[]{:S(2)}, u32[]{:S(2)}) collective-permute-start(f32[1,4,1,512]{3,2,1,0:T(1,128)S(1)} %get-tuple-element.35), channel_id=1, source_target_pairs={{2,0},{4,2},{6,4},{3,1},{5,3},{7,5},{10,8},{12,10},{14,12},{11,9},... | collective-permute-start | bytes 24584 | tf_op jit(solution)/shard_map/ppermute | solution.py:28
  227.1 4.1 %collective-permute-start.28 = (f32[1,4,66,1]{3,2,1,0:T(8,128)S(1)}, f32[1,4,66,1]{3,2,1,0:T(8,128)S(1)}, u32[]{:S(2)}, u32[]{:S(2)}) collective-permute-start(f32[1,4,66,1]{3,2,1,0:T(8,128)S(1)} %get-tuple-element.22), channel_id=1, source_target_pairs={{0,1},{2,3},{4,5},{6,7},{8,9},{10,11},{12,13},{14,15},{16,17},{18,... | collective-permute-start | bytes 3176 | tf_op jit(solution)/shard_map/ppermute | solution.py:26
  228.6 7.0 %collective-permute-start.29 = (f32[1,4,66,1]{3,2,1,0:T(8,128)S(1)}, f32[1,4,66,1]{3,2,1,0:T(8,128)S(1)}, u32[]{:S(2)}, u32[]{:S(2)}) collective-permute-start(f32[1,4,66,1]{3,2,1,0:T(8,128)S(1)} %get-tuple-element.23), channel_id=1, source_target_pairs={{1,0},{3,2},{5,4},{7,6},{9,8},{11,10},{13,12},{15,14},{17,16},{19,... | collective-permute-start | bytes 3176 | tf_op jit(solution)/shard_map/ppermute | solution.py:28
  305.0 28.6 %copy-start.3 = (f32[2,64,512]{2,1,0:T(8,128)S(1)}, f32[2,64,512]{2,1,0:T(8,128)}, u32[]{:S(2)}) copy-start(f32[2,64,512]{2,1,0:T(8,128)} %copy-done.1) | copy-start | bytes 786436
  305.0 28.6 %copy-start.7 = (f32[2,64,512]{2,1,0:T(8,128)S(1)}, f32[2,64,512]{2,1,0:T(8,128)}, u32[]{:S(2)}) copy-start(f32[2,64,512]{2,1,0:T(8,128)} %copy-done.5) | copy-start | bytes 786436
  334.8 27.5 %copy-start.15 = (f32[1,2,64,512]{3,2,1,0:T(8,128)}, f32[1,2,64,512]{3,2,1,0:T(8,128)S(1)}, u32[]{:S(2)}) copy-start(f32[1,2,64,512]{3,2,1,0:T(8,128)S(1)} %fusion.207) | copy-start | bytes 786436
  334.8 7.7 %collective-permute-start.30 = (f32[1,1,64,512]{3,2,1,0:T(8,128)S(1)}, f32[1,1,64,512]{3,2,1,0:T(8,128)S(1)}, u32[]{:S(2)}, u32[]{:S(2)}) collective-permute-start(f32[1,1,64,512]{3,2,1,0:T(8,128)S(1)} %get-tuple-element.46), channel_id=1, source_target_pairs={{0,8},{8,16},{16,24},{1,9},{9,17},{17,25},{2,10},{10,18},{18,26},{... | collective-permute-start | bytes 393224 | tf_op jit(solution)/shard_map/ppermute | solution.py:26
  336.8 6.1 %collective-permute-start.31 = (f32[1,1,64,512]{3,2,1,0:T(8,128)S(1)}, f32[1,1,64,512]{3,2,1,0:T(8,128)S(1)}, u32[]{:S(2)}, u32[]{:S(2)}) collective-permute-start(f32[1,1,64,512]{3,2,1,0:T(8,128)S(1)} %get-tuple-element.47), channel_id=1, source_target_pairs={{8,0},{16,8},{24,16},{9,1},{17,9},{25,17},{10,2},{18,10},{26,18},{... | collective-permute-start | bytes 393224 | tf_op jit(solution)/shard_map/ppermute | solution.py:28
  342.5 19.8 %copy-start.25 = (f32[1,1,64,512]{3,2,1,0:T(8,128)}, f32[1,1,64,512]{3,2,1,0:T(8,128)S(1)}, u32[]{:S(2)}) copy-start(f32[1,1,64,512]{3,2,1,0:T(8,128)S(1)} %collective-permute-done.30) | copy-start | bytes 393220
  342.9 19.4 %copy-start.26 = (f32[1,1,64,512]{3,2,1,0:T(8,128)}, f32[1,1,64,512]{3,2,1,0:T(8,128)S(1)}, u32[]{:S(2)}) copy-start(f32[1,1,64,512]{3,2,1,0:T(8,128)S(1)} %collective-permute-done.31) | copy-start | bytes 393220
  342.9 3.8 collective-permute-start.32
  344.2 5.5 %collective-permute-start.33 = (f32[1,4,1,512]{3,2,1,0:T(1,128)S(1)}, f32[1,4,1,512]{3,2,1,0:T(1,128)S(1)}, u32[]{:S(2)}, u32[]{:S(2)}) collective-permute-start(f32[1,4,1,512]{3,2,1,0:T(1,128)S(1)} %get-tuple-element.33), channel_id=1, source_target_pairs={{2,0},{4,2},{6,4},{3,1},{5,3},{7,5},{10,8},{12,10},{14,12},{11,9},... | collective-permute-start | bytes 24584 | tf_op jit(solution)/shard_map/ppermute | solution.py:28
  350.6 11.7 %collective-permute-start.34 = (f32[1,4,66,1]{3,2,1,0:T(8,128)}, f32[1,4,66,1]{3,2,1,0:T(8,128)S(1)}, u32[]{:S(2)}, u32[]{:S(2)}) collective-permute-start(f32[1,4,66,1]{3,2,1,0:T(8,128)} %get-tuple-element.20), channel_id=1, source_target_pairs={{0,1},{2,3},{4,5},{6,7},{8,9},{10,11},{12,13},{14,15},{16,17},{18,... | collective-permute-start | bytes 3176 | tf_op jit(solution)/shard_map/ppermute | solution.py:26
  354.5 8.9 %collective-permute-start.35 = (f32[1,4,66,1]{3,2,1,0:T(8,128)}, f32[1,4,66,1]{3,2,1,0:T(8,128)}, u32[]{:S(2)}, u32[]{:S(2)}) collective-permute-start(f32[1,4,66,1]{3,2,1,0:T(8,128)} %get-tuple-element.21), channel_id=1, source_target_pairs={{1,0},{3,2},{5,4},{7,6},{9,8},{11,10},{13,12},{15,14},{17,16},{19,... | collective-permute-start | bytes 3176 | tf_op jit(solution)/shard_map/ppermute | solution.py:28
  367.4 11.2 %collective-permute-start.36 = (f32[1,1,64,512]{3,2,1,0:T(8,128)}, f32[1,1,64,512]{3,2,1,0:T(8,128)}, u32[]{:S(2)}, u32[]{:S(2)}) collective-permute-start(f32[1,1,64,512]{3,2,1,0:T(8,128)} %get-tuple-element.44), channel_id=1, source_target_pairs={{0,8},{8,16},{16,24},{1,9},{9,17},{17,25},{2,10},{10,18},{18,26},{... | collective-permute-start | bytes 393224 | tf_op jit(solution)/shard_map/ppermute | solution.py:26
  369.3 9.3 %collective-permute-start.37 = (f32[1,1,64,512]{3,2,1,0:T(8,128)}, f32[1,1,64,512]{3,2,1,0:T(8,128)}, u32[]{:S(2)}, u32[]{:S(2)}) collective-permute-start(f32[1,1,64,512]{3,2,1,0:T(8,128)} %get-tuple-element.45), channel_id=1, source_target_pairs={{8,0},{16,8},{24,16},{9,1},{17,9},{25,17},{10,2},{18,10},{26,18},{... | collective-permute-start | bytes 393224 | tf_op jit(solution)/shard_map/ppermute | solution.py:28
  378.5 20.0 %copy-start.18 = (f32[1,2,64,512]{3,2,1,0:T(8,128)S(1)}, f32[1,2,64,512]{3,2,1,0:T(8,128)}, u32[]{:S(2)}) copy-start(f32[1,2,64,512]{3,2,1,0:T(8,128)} %copy-done.16) | copy-start | bytes 786436
  379.4 5.2 %collective-permute-start.38 = (f32[1,4,1,512]{3,2,1,0:T(1,128)S(1)}, f32[1,4,1,512]{3,2,1,0:T(1,128)S(1)}, u32[]{:S(2)}, u32[]{:S(2)}) collective-permute-start(f32[1,4,1,512]{3,2,1,0:T(1,128)S(1)} %get-tuple-element.30), channel_id=1, source_target_pairs={{0,2},{2,4},{4,6},{1,3},{3,5},{5,7},{8,10},{10,12},{12,14},{9,11},... | collective-permute-start | bytes 24584 | tf_op jit(solution)/shard_map/ppermute | solution.py:26
  381.1 5.5 %collective-permute-start.39 = (f32[1,4,1,512]{3,2,1,0:T(1,128)S(1)}, f32[1,4,1,512]{3,2,1,0:T(1,128)S(1)}, u32[]{:S(2)}, u32[]{:S(2)}) collective-permute-start(f32[1,4,1,512]{3,2,1,0:T(1,128)S(1)} %get-tuple-element.31), channel_id=1, source_target_pairs={{2,0},{4,2},{6,4},{3,1},{5,3},{7,5},{10,8},{12,10},{14,12},{11,9},... | collective-permute-start | bytes 24584 | tf_op jit(solution)/shard_map/ppermute | solution.py:28
  387.6 6.6 %collective-permute-start.40 = (f32[1,4,66,1]{3,2,1,0:T(8,128)S(1)}, f32[1,4,66,1]{3,2,1,0:T(8,128)S(1)}, u32[]{:S(2)}, u32[]{:S(2)}) collective-permute-start(f32[1,4,66,1]{3,2,1,0:T(8,128)S(1)} %get-tuple-element.18), channel_id=1, source_target_pairs={{0,1},{2,3},{4,5},{6,7},{8,9},{10,11},{12,13},{14,15},{16,17},{18,... | collective-permute-start | bytes 3176 | tf_op jit(solution)/shard_map/ppermute | solution.py:26
  391.5 7.0 %collective-permute-start.41 = (f32[1,4,66,1]{3,2,1,0:T(8,128)S(1)}, f32[1,4,66,1]{3,2,1,0:T(8,128)S(1)}, u32[]{:S(2)}, u32[]{:S(2)}) collective-permute-start(f32[1,4,66,1]{3,2,1,0:T(8,128)S(1)} %get-tuple-element.19), channel_id=1, source_target_pairs={{1,0},{3,2},{5,4},{7,6},{9,8},{11,10},{13,12},{15,14},{17,16},{19,... | collective-permute-start | bytes 3176 | tf_op jit(solution)/shard_map/ppermute | solution.py:28
  (41 other events, 384.9 us)
